TPU v7x, 32 devices: a whole 2x2x4 slice. The times are simulated.
32 devices in a mesh: grp: 2 (over x), tile: 16 (over z, y, core).
Axes of the slice: x: 2, y: 2, z: 4, core: 2. Of those that a mesh axis runs over, the one named last changes fastest.
Arguments:
- latent: float32 [32, 1024, 128], P(None, ('grp', 'tile')), parts along dimension 1, may hold values from -6 to 6
- observed: float32 [32, 1024, 128], P(None, ('grp', 'tile')), parts along dimension 1, may hold values from -6 to 6
- noise: float32 [32, 1024, 128], P(None, ('grp', 'tile')), parts along dimension 1, may hold values from -6 to 6
- cloudy: int32 [128], P(('grp', 'tile')), parts along dimension 0, may hold values from 0 to 1, as said below
- timestep: int32 [2], P('grp'), parts along dimension 0, may hold values from 200 to 800
- pos_embed: bfloat16 [256, 2048], replicated, may hold values from -3 to 3
- embed_w: bfloat16 [128, 2048], replicated, may hold values from -0.5 to 0.5
- mod_w: bfloat16 [256, 6144], P(None, 'tile'), may hold values from -0.375 to 0.375
- wq: bfloat16 [2048, 1024], P('tile')
- wk: bfloat16 [2048, 1024], P('tile')
- wv: bfloat16 [2048, 1024], P('tile'), may hold values from -0.125 to 0.125
- wo: bfloat16 [1024, 2048], P(None, 'tile'), may hold values from -0.1875 to 0.1875
- q_gain: float32 [128], replicated, may hold values from 0.6 to 4.2
- k_gain: float32 [128], replicated, may hold values from 0.6 to 4.2
- out_w: bfloat16 [2048, 128], replicated, may hold values from -0.125 to 0.125
- conv_w: float32 [9, 32, 32], replicated, may hold values from -0.375 to 0.375
Outputs:
- estimate: float32 [32, 1024, 128], P(None, ('grp', 'tile')), parts along dimension 1
- next_latent: float32 [32, 1024, 128], P(None, ('grp', 'tile')), parts along dimension 1
There are 2 independent parts, one for each index of `grp`. A program takes and returns all parts, laid end to end along the dimension named above; an argument that names none is the same for every part. Nothing has to cross between parts.
Inputs may be any that keep to these rules, and one draw needn't show every extreme that they name: Exactly 16 tiles of a part are cloudy; each band of 4 tiles holds at most 3 of them, and some band holds exactly 3.
All inputs are finite; a program needn't handle non-finite values.
Results may differ from a plain program's by a relative error of at most 0.0033.
Values may be sent and summed in bfloat16 or wider, within the bound.
No kernel may reach another device: no remote copies, remote signals or barrier semaphores. Data moves between devices by JAX's collectives and lax.ppermute only.
A program may use at most 128 MiB of HBM per device.

v0:
```python
import math

import jax
import jax.numpy as jnp
from jax import lax
from jax.sharding import PartitionSpec as P

HD = 128
PATCH = 2
MAXOWN = 3
TSTEPS = 1000
STRIDE = 20


def padded_2(block, sides, width):
    for axis, dim in sides:
        count = lax.axis_size(axis)
        forward = [(i, i + 1) for i in range(count - 1)]
        backward = [(target, source) for source, target in forward]
        low = lax.ppermute(
            lax.slice_in_dim(block, block.shape[dim] - width, None, axis=dim), axis, forward
        )
        high = lax.ppermute(lax.slice_in_dim(block, 0, width, axis=dim), axis, backward)
        block = jnp.concatenate([low, block, high], axis=dim)
    return block


def plan(step):
    theta = (step / TSTEPS + 0.008) / 1.008 * (math.pi / 2)
    return (jnp.cos(theta), jnp.sin(theta))


def time_features(step, width):
    half = width // 2
    freqs = jnp.exp(-math.log(10000.0) * jnp.arange(half, dtype=jnp.float32) / half)
    angles = step * freqs
    code = jnp.concatenate([jnp.cos(angles), jnp.sin(angles)])[None, :]
    return jax.nn.silu(code).astype(jnp.bfloat16)


def layer_norm(values):
    center = values - jnp.mean(values, axis=-1, keepdims=True)
    spread = jnp.mean(center * center, axis=-1, keepdims=True)
    return center * lax.rsqrt(spread + 1e-06)


def head_norm(proj, gain, count, tokens_tile):
    shaped = proj.reshape(count, tokens_tile, -1, HD)
    scaled = shaped * lax.rsqrt(jnp.mean(shaped * shaped, axis=-1, keepdims=True) + 1e-06)
    return (scaled * gain).astype(jnp.bfloat16)


def band_tiles(band, tile_side):
    channels, band_rows, band_cols = band.shape
    tiles_here = band_cols // (tile_side * PATCH)
    shaped = band.reshape(channels, tile_side, PATCH, tiles_here, tile_side, PATCH)
    return jnp.transpose(shaped, (3, 1, 4, 2, 5, 0)).reshape(
        tiles_here, tile_side * tile_side, PATCH * PATCH * channels
    )


def band_pixels(tiled, tile_side, channels):
    tiles_here = tiled.shape[0]
    shaped = tiled.reshape(tiles_here, tile_side, tile_side, PATCH, PATCH, channels)
    return jnp.transpose(shaped, (5, 1, 3, 0, 2, 4)).reshape(
        channels, tile_side * PATCH, tiles_here * tile_side * PATCH
    )


def add_rows(left, shard_rows):
    return jnp.dot(left, shard_rows, preferred_element_type=jnp.float32)


def denoise(
    chosen,
    embed_w,
    pos_embed,
    shift_vec,
    scale_vec,
    gate_vec,
    wq,
    wk,
    wv,
    wo,
    q_gain,
    k_gain,
    out_w,
):
    count, tokens_tile, token_values = chosen.shape
    row_count = count * tokens_tile
    flat = chosen.reshape(row_count, token_values)
    hidden0 = jnp.dot(flat, embed_w, preferred_element_type=jnp.float32).reshape(
        count, tokens_tile, -1
    )
    hidden0 = (hidden0 + pos_embed.astype(jnp.float32)[None]).reshape(row_count, -1)
    modulated = (layer_norm(hidden0) * (1.0 + scale_vec) + shift_vec).astype(jnp.bfloat16)

    def add_one(shard_rows):
        return add_rows(modulated, shard_rows)

    query_all = add_one(lax.all_gather(wq, "tile", axis=0, tiled=True))
    key_all = add_one(lax.all_gather(wk, "tile", axis=0, tiled=True))
    value_all = add_one(lax.all_gather(wv, "tile", axis=0, tiled=True))
    query_norm = head_norm(query_all, q_gain, count, tokens_tile)
    key_norm = head_norm(key_all, k_gain, count, tokens_tile)
    value_half = value_all.reshape(count, tokens_tile, -1, HD).astype(jnp.bfloat16)
    scores = jnp.einsum(
        "nqhd,nkhd->nhqk", query_norm, key_norm, preferred_element_type=jnp.float32
    ) * HD ** (-0.5)
    peak = jnp.max(scores, axis=-1, keepdims=True)
    expo = jnp.exp(scores - peak)
    probs = (expo / jnp.sum(expo, axis=-1, keepdims=True)).astype(jnp.bfloat16)
    mixed = jnp.einsum("nhqk,nkhd->nqhd", probs, value_half, preferred_element_type=jnp.float32)
    mixed = mixed.astype(jnp.bfloat16).reshape(row_count, -1)
    attn_out = jnp.dot(
        mixed, lax.all_gather(wo, "tile", axis=1, tiled=True), preferred_element_type=jnp.float32
    )
    hidden1 = hidden0 + gate_vec * attn_out
    final = layer_norm(hidden1).astype(jnp.bfloat16)
    eps_pred = jnp.dot(final, out_w, preferred_element_type=jnp.float32).astype(jnp.bfloat16)
    return eps_pred.reshape(count, tokens_tile, token_values)


def on_device(
    latent,
    observed,
    noise,
    cloudy,
    timestep,
    pos_embed,
    embed_w,
    mod_w,
    wq,
    wk,
    wv,
    wo,
    q_gain,
    k_gain,
    out_w,
    conv_w,
):
    channels, band_rows, band_cols = latent.shape
    tile_side = band_rows // PATCH
    tiles_here = band_cols // band_rows
    width = embed_w.shape[1]
    step_now = timestep[0].astype(jnp.float32)
    cos_now, sin_now = plan(step_now)
    cos_prev, sin_prev = plan(step_now - STRIDE)
    time_code = time_features(step_now, mod_w.shape[0])
    local_mod = jnp.dot(time_code, mod_w, preferred_element_type=jnp.float32)
    modulation = lax.all_gather(local_mod, "tile", axis=1, tiled=True)
    shift_vec = modulation[:, :width]
    scale_vec = modulation[:, width : 2 * width]
    gate_vec = modulation[:, 2 * width :]
    tile_tokens = band_tiles(latent.astype(jnp.bfloat16), tile_side)
    order_in = jnp.cumsum(cloudy) - cloudy
    weights_all = (
        embed_w,
        pos_embed,
        shift_vec,
        scale_vec,
        gate_vec,
        wq,
        wk,
        wv,
        wo,
        q_gain,
        k_gain,
        out_w,
    )
    slot_ids = jnp.arange(MAXOWN, dtype=jnp.int32)
    slot_hit = (cloudy[None, :] == 1) & (order_in[None, :] == slot_ids[:, None])
    picked = jnp.sum(
        jnp.where(slot_hit, jnp.arange(tiles_here, dtype=jnp.int32)[None, :], 0), axis=1
    )
    chosen = jnp.take(tile_tokens, picked, axis=0)
    eps_chosen = denoise(chosen, *weights_all)
    eps_back = jnp.take(eps_chosen, jnp.minimum(order_in, MAXOWN - 1), axis=0)
    eps_tiles = jnp.where(cloudy[:, None, None] == 1, eps_back, jnp.zeros_like(eps_back))
    eps_latent = band_pixels(eps_tiles.astype(jnp.float32), tile_side, channels)
    cloud_cols = jnp.repeat(cloudy, band_rows) == 1
    raw_estimate = jnp.where(
        cloud_cols[None, None, :], (latent - sin_now * eps_latent) / cos_now, observed
    )
    padded = padded_2(raw_estimate, (("tile", 1),), 1)
    padded = jnp.pad(padded, ((0, 0), (0, 0), (1, 1)))
    blended = jnp.zeros_like(raw_estimate)
    for row_shift in range(3):
        for col_shift in range(3):
            window = padded[:, row_shift : row_shift + band_rows, col_shift : col_shift + band_cols]
            blended = blended + jnp.einsum(
                "oc,chw->ohw",
                conv_w[3 * row_shift + col_shift],
                window,
                precision=lax.Precision.HIGHEST,
            )
    row_pos = jnp.arange(band_rows) % band_rows
    col_pos = jnp.arange(band_cols) % band_rows
    seam_mask = ((row_pos == 0) | (row_pos == band_rows - 1))[:, None] | (
        (col_pos == 0) | (col_pos == band_rows - 1)
    )[None, :]
    estimate = jnp.where(seam_mask[None], blended, raw_estimate)
    next_latent = cos_prev * estimate + sin_prev * noise
    return (estimate, next_latent)


def solution(mesh):
    placed = (
        P(None, ("grp", "tile"), None),
        P(None, ("grp", "tile"), None),
        P(None, ("grp", "tile"), None),
        P(("grp", "tile")),
        P("grp"),
        P(),
        P(),
        P(None, "tile"),
        P("tile", None),
        P("tile", None),
        P("tile", None),
        P(None, "tile"),
        P(),
        P(),
        P(),
        P(),
    )
    return jax.shard_map(
        on_device,
        mesh=mesh,
        in_specs=placed,
        out_specs=(P(None, ("grp", "tile"), None), P(None, ("grp", "tile"), None)),
        check_vma=False,
    )
```

profile of v0, /device:TPU:1, one launch (start us, length us, event | category | flops | bytes accessed | tf_op | source)
XLA Modules:
  0.0 257.6 jit_solution(8507005595487570797)
XLA Ops:
  12.3 1.1 convolution_bitcast_fusion
  13.6 1.5 copy.77
  15.1 1.1 copy.78
  16.8 1.5 convert_element_type.57
  19.0 23.0 %all-gather.1 = f32[16,1,384]{2,1,0:T(1,128)S(1)} all-gather(f32[1,1,384]{2,1,0:T(1,128)S(1)} %convolution_bitcast_fusion), channel_id=2, replica_groups=mesh['grp'=2,'tile'=16] {'tile'}, dimensions={0}, use_global_device_ids=true | all-gather | bytes 26112 | tf_op jit(solution)/shard_map/all_gather | solution.py:151
  42.1 1.1 fusion.72
  44.0 1.8 copy-done.2
  45.8 2.8 %fusion.4 = bf16[3,256,2048,1]{2,1,3,0:T(8,128)(2,1)} fusion(f32[3,256,2048]{2,1,0:T(8,128)S(1)} %get-tuple-element.22, f32[2048]{0:T(1024)S(1)} %bitcast.119, f32[2048]{0:T(1024)S(1)} %bitcast.118, f32[3,256]{1,0:T(4,128)S(1)} %add_rsqrt_fusion.3, f32[3,256]{1,0:T(4,128)S(1)} %broadcast_multiply_fusion.1), kind=kLoop, calls=%fused_computation.13 | loop fusion | flops 7864320 | bytes 9459712 | tf_op jit(solution)/shard_map/convert_element_type | solution.py:96
  48.7 14.8 %all-gather.11.cloned.1.call-done = bf16[2048,1024]{1,0:T(8,128)(2,1)} async-done(((bf16[128,1024]{1,0:T(8,128)(2,1)}), bf16[2048,1024]{1,0:T(8,128)(2,1)}) %all-gather.11.cloned.1.call-update) | async-done | bytes 4194320 | tf_op jit(solution)/shard_map/all_gather | solution.py:102
  63.5 6.5 %copy.81 = bf16[1024,2048]{1,0:T(8,128)(2,1)} copy(bf16[1024,2048]{0,1:T(8,128)(2,1)} %bitcast.108) | data formatting | bytes 8388608 | tf_op jit(solution)/shard_map/dot_general | solution.py:71
  70.0 44.7 %all-gather.9.cloned.1.call-done = bf16[2048,1024]{1,0:T(8,128)(2,1)} async-done(((bf16[128,1024]{1,0:T(8,128)(2,1)}), bf16[2048,1024]{1,0:T(8,128)(2,1)}) %all-gather.9.cloned.1.call-update) | async-done | bytes 4194320 | tf_op jit(solution)/shard_map/all_gather | solution.py:101
  114.7 6.5 %copy.80 = bf16[1024,2048]{1,0:T(8,128)(2,1)} copy(bf16[1024,2048]{0,1:T(8,128)(2,1)} %bitcast.109) | data formatting | bytes 8388608 | tf_op jit(solution)/shard_map/dot_general | solution.py:71
  121.2 44.7 %all-gather.7.cloned.1.call-done = bf16[2048,1024]{1,0:T(8,128)(2,1)} async-done(((bf16[128,1024]{1,0:T(8,128)(2,1)}), bf16[2048,1024]{1,0:T(8,128)(2,1)}) %all-gather.7.cloned.1.call-update) | async-done | bytes 4194320 | tf_op jit(solution)/shard_map/all_gather | solution.py:103
  166.0 6.5 %copy.79 = bf16[1024,2048]{1,0:T(8,128)(2,1)} copy(bf16[1024,2048]{0,1:T(8,128)(2,1)} %bitcast.110) | data formatting | bytes 8388608 | tf_op jit(solution)/shard_map/dot_general | solution.py:71
  172.4 6.6 %multiply_reduce_fusion.3 = (f32[3,256,8]{1,2,0:T(8,128)S(1)}, f32[3,256,8,128]{1,3,2,0:T(8,128)S(1)}) fusion(bf16[3,256,2048,1]{2,1,3,0:T(8,128)(2,1)} %fusion.4, bf16[8,128,2048,1]{2,1,0,3:T(8,128)(2,1)} %bitcast.113), kind=kOutput, calls=%fused_computation.19 | convolution fusion | flops 3222792192 | bytes 10510336 | tf_op jit(solution)/shard_map/dot_general | solution.py:71
  179.1 3.5 %multiply_reduce_fusion.4 = (f32[3,256,8]{1,2,0:T(8,128)S(1)}, f32[3,256,8,128]{1,3,2,0:T(8,128)S(1)}) fusion(bf16[3,256,2048,1]{2,1,3,0:T(8,128)(2,1)S(1)} %copy-done.4, bf16[8,128,2048,1]{2,1,0,3:T(8,128)(2,1)S(1)} %bitcast.112), kind=kOutput, calls=%fused_computation.21 | convolution fusion | flops 3222792192 | bytes 10510336 | tf_op jit(solution)/shard_map/dot_general | solution.py:71
  182.6 1.3 fusion.11
  183.9 4.3 %fusion.73 = (f32[3,8,256]{2,1,0:T(8,128)S(1)}, f32[3,8,256,256]{2,3,1,0:T(8,128)}) fusion(f32[3,8,256,256]{2,3,1,0:T(8,128)S(1)} %fusion.11), kind=kOutput, calls=%fused_computation.131 | output fusion | flops 6291711 | bytes 12607488 | tf_op jit(solution)/shard_map/sub | solution.py:111
  188.2 10.3 %fusion.18 = bf16[3,256,8,128]{1,3,2,0:T(8,128)(2,1)} fusion(f32[3,8,256,256]{2,3,1,0:T(8,128)} %get-tuple-element.28, f32[3,8,256]{2,1,0:T(8,128)S(1)} %get-tuple-element.27, bf16[3,256,2048,1]{2,1,3,0:T(8,128)(2,1)} %fusion.4, bf16[8,128,2048,1]{2,1,0,3:T(8,128)(2,1)} %bitcast.111), kind=kOutput, calls=%fused_computation.37 | convolution fusion | flops 3628597248 | bytes 15228928 | tf_op jit(solution)/shard_map/nhqk,nkhd->nqhd/dot_general | solution.py:113
  198.5 2.0 copy.86
  200.5 19.2 %all-gather.13.cloned.1.call-done = bf16[1024,2048]{1,0:T(8,128)(2,1)} async-done(((bf16[1024,128]{1,0:T(8,128)(2,1)}), bf16[1024,2048]{1,0:T(8,128)(2,1)}) %all-gather.13.cloned.1.call-update) | async-done | bytes 4194320 | tf_op jit(solution)/shard_map/all_gather | solution.py:116
  219.7 7.0 %fusion.74 = (f32[768]{0:T(1024)S(1)}, f32[768,2048]{1,0:T(8,128)S(1)}) fusion(bf16[1024,2048]{1,0:T(8,128)(2,1)} %all-gather.13.cloned.1.call-done, bf16[96,8,8,128]{3,2,1,0:T(8,128)(2,1)S(1)} %bitcast.115, f32[2048]{0:T(1024)S(1)} %bitcast.120, f32[3,256,2048]{2,1,0:T(8,128)} %copy-done.2), kind=kOutput, calls=%fused_computation.132 | convolution fusion | flops 3225943296 | bytes 18361344 | tf_op jit(solution)/shard_map/dot_general | solution.py:115
  227.8 1.1 fusion.22
  229.9 1.1 multiply_bitcast_fusion
  231.0 1.1 copy.87
  232.7 1.6 copy_select_fusion
  234.4 3.2 %collective-permute-start = (f32[32,1,128]{2,0,1:T(8,128)S(1)}, f32[32,1,128]{2,0,1:T(8,128)S(1)}, u32[]{:S(2)}, u32[]{:S(2)}) collective-permute-start(f32[32,1,128]{2,0,1:T(8,128)S(1)} %get-tuple-element.15), channel_id=1, source_target_pairs={{0,1},{1,2},{2,3},{3,4},{4,5},{5,6},{6,7},{7,8},{8,9},{9,10},{10,1... | collective-permute-start | bytes 49160 | tf_op jit(solution)/shard_map/ppermute | solution.py:20
  237.5 2.2 collective-permute-start.1
  240.0 2.6 %collective-permute-done.1 = f32[32,1,128]{2,0,1:T(8,128)S(1)} collective-permute-done((f32[32,1,128]{2,0,1:T(8,128)S(1)}, f32[32,1,128]{2,0,1:T(8,128)S(1)}, u32[]{:S(2)}, u32[]{:S(2)}) %collective-permute-start.1) | collective-permute-done | bytes 16416 | tf_op jit(solution)/shard_map/ppermute | solution.py:23
  248.0 0.9 fusion.39
  248.9 1.1 copy.92
  250.0 1.1 copy.93
  (69 shorter events, 14.6 us)
Async XLA Ops:
  7.2 34.9 %copy-start = (bf16[128,2048]{1,0:T(8,128)(2,1)S(1)}, bf16[128,2048]{1,0:T(8,128)(2,1)}, u32[]{:S(2)}) copy-start(bf16[128,2048]{1,0:T(8,128)(2,1)} %param.22) | copy-start | bytes 1572868
  7.2 56.3 %all-gather.11.cloned.1.call-start = ((), (), s32[]{:S(2)}) async-start(), calls=%async_computation.2 | async-start | bytes 4456448 | tf_op jit(solution)/shard_map/all_gather | solution.py:102
  7.9 106.8 %all-gather.9.cloned.1.call-start = ((), (), s32[]{:S(2)}) async-start(), calls=%async_computation.1 | async-start | bytes 4456448 | tf_op jit(solution)/shard_map/all_gather | solution.py:101
  8.7 157.3 %all-gather.7.cloned.1.call-start = ((), (), s32[]{:S(2)}) async-start(), calls=%async_computation | async-start | bytes 4456448 | tf_op jit(solution)/shard_map/all_gather | solution.py:103
  9.4 210.3 %all-gather.13.cloned.1.call-start = ((), (), s32[]{:S(2)}) async-start(), calls=%async_computation.3 | async-start | bytes 4456448 | tf_op jit(solution)/shard_map/all_gather | solution.py:116
  43.2 2.7 %copy-start.2 = (f32[3,256,2048]{2,1,0:T(8,128)}, f32[3,256,2048]{2,1,0:T(8,128)S(1)}, u32[]{:S(2)}) copy-start(f32[3,256,2048]{2,1,0:T(8,128)S(1)} %get-tuple-element.22) | copy-start | bytes 18874372
  172.4 6.7 %copy-start.3 = (bf16[1024,2048]{1,0:T(8,128)(2,1)S(1)}, bf16[1024,2048]{1,0:T(8,128)(2,1)}, u32[]{:S(2)}) copy-start(bf16[1024,2048]{1,0:T(8,128)(2,1)} %copy.80) | copy-start | bytes 12582916
  172.4 6.7 %copy-start.4 = (bf16[3,256,2048,1]{2,1,3,0:T(8,128)(2,1)S(1)}, bf16[3,256,2048,1]{2,1,3,0:T(8,128)(2,1)}, u32[]{:S(2)}) copy-start(bf16[3,256,2048,1]{2,1,3,0:T(8,128)(2,1)} %fusion.4) | copy-start | bytes 9437188
  179.1 3.5 %copy-start.9 = (f32[128]{0:T(128)S(1)}, f32[128]{0:T(128)}, u32[]{:S(2)}) copy-start(f32[128]{0:T(128)} %param.29) | copy-start | bytes 1540
  179.1 3.5 %copy-start.10 = (f32[128]{0:T(128)S(1)}, f32[128]{0:T(128)}, u32[]{:S(2)}) copy-start(f32[128]{0:T(128)} %param.28) | copy-start | bytes 1540
  226.7 1.0 copy-start.7
  230.9 1.8 copy-start.5
  232.1 10.8 %copy-start.8 = (f32[9,32,32]{2,1,0:T(8,128)S(1)}, f32[9,32,32]{2,1,0:T(8,128)}, u32[]{:S(2)}) copy-start(f32[9,32,32]{2,1,0:T(8,128)} %param.31) | copy-start | bytes 110596
  234.4 5.6 %collective-permute-start = (f32[32,1,128]{2,0,1:T(8,128)S(1)}, f32[32,1,128]{2,0,1:T(8,128)S(1)}, u32[]{:S(2)}, u32[]{:S(2)}) collective-permute-start(f32[32,1,128]{2,0,1:T(8,128)S(1)} %get-tuple-element.15), channel_id=1, source_target_pairs={{0,1},{1,2},{2,3},{3,4},{4,5},{5,6},{6,7},{7,8},{8,9},{9,10},{10,1... | collective-permute-start | bytes 49160 | tf_op jit(solution)/shard_map/ppermute | solution.py:20
  237.5 5.1 %collective-permute-start.1 = (f32[32,1,128]{2,0,1:T(8,128)S(1)}, f32[32,1,128]{2,0,1:T(8,128)S(1)}, u32[]{:S(2)}, u32[]{:S(2)}) collective-permute-start(f32[32,1,128]{2,0,1:T(8,128)S(1)} %get-tuple-element.16), channel_id=1, source_target_pairs={{1,0},{2,1},{3,2},{4,3},{5,4},{6,5},{7,6},{8,7},{9,8},{10,9},{11,1... | collective-permute-start | bytes 49160 | tf_op jit(solution)/shard_map/ppermute | solution.py:23
  245.5 2.5 copy-start.6
  247.4 3.7 %copy-start.1 = (bf16[128,2048]{1,0:T(8,128)(2,1)S(1)}, bf16[128,2048]{1,0:T(8,128)(2,1)}, u32[]{:S(2)}) copy-start(bf16[128,2048]{1,0:T(8,128)(2,1)} %param.22) | copy-start | bytes 1572868
Sparse Core Ops, SparseCore 0:
  10.2 53.2 all-gather.10
  65.6 49.0 all-gather.8
  116.9 49.0 all-gather.6
  168.0 51.7 all-gather.12
where the time goes:
time: 258 us
  waiting for transfers between devices  129 us (50%)
  matrix products  37.7 us (15%)
  local copies, waits for them, and re-layouts  32.5 us (13%)
  blocking collectives  23 us (9%)
  between operations  15.2 us (6%)
  other arithmetic  15 us (6%)
  starting transfers between devices  5.5 us (2%)
    all_gather x1, waiting for transfers between devices, denoise(): value_all = add_one(lax.all_gather(wv, 'tile', axis=0, tiled=True))  44.7 us
    all_gather x1, waiting for transfers between devices, denoise(): query_all = add_one(lax.all_gather(wq, 'tile', axis=0, tiled=True))  44.7 us
    all_gather x1, blocking collectives, on_device(): modulation = lax.all_gather(local_mod, 'tile', axis=1, tiled=True)  23 us
    dot_general x3, local copies, waits for them, and re-layouts, add_rows(): return jnp.dot(left, shard_rows, preferred_element_type=jnp.float32)  19.5 us
    all_gather x1, waiting for transfers between devices, denoise(): lax.all_gather(wo, 'tile', axis=1, tiled=True)  19.2 us
    all_gather x1, waiting for transfers between devices, denoise(): key_all = add_one(lax.all_gather(wk, 'tile', axis=0, tiled=True))  14.8 us
    dot_general x1, matrix products, denoise(): jnp.einsum('nhqk,nkhd->nqhd', probs, value_half, preferred_element_type=j...  10.3 us
    dot_general x2, matrix products, add_rows(): return jnp.dot(left, shard_rows, preferred_element_type=jnp.float32)  10.1 us
  transfers between devices with their start and end apart: 6, of which 5 were waited for; matrix products, arithmetic and copies ran while one was open for 23% of the time, Pallas kernels for 0%

commit v1 on v0

--- a/solution.py
+++ b/solution.py
@@ -98,9 +98,12 @@
     def add_one(shard_rows):
         return add_rows(modulated, shard_rows)
 
-    query_all = add_one(lax.all_gather(wq, "tile", axis=0, tiled=True))
-    key_all = add_one(lax.all_gather(wk, "tile", axis=0, tiled=True))
-    value_all = add_one(lax.all_gather(wv, "tile", axis=0, tiled=True))
+    inner = wq.shape[1]
+    qkv = lax.all_gather(jnp.concatenate([wq, wk, wv], axis=1), "tile", axis=0, tiled=True)
+    qkv_all = add_one(qkv)
+    query_all = qkv_all[:, :inner]
+    key_all = qkv_all[:, inner : 2 * inner]
+    value_all = qkv_all[:, 2 * inner :]
     query_norm = head_norm(query_all, q_gain, count, tokens_tile)
     key_norm = head_norm(key_all, k_gain, count, tokens_tile)
     value_half = value_all.reshape(count, tokens_tile, -1, HD).astype(jnp.bfloat16)

time: 258 us -> 206 us (0.80)
  waiting for transfers between devices: 129 us -> 72.9 us
  other arithmetic: 15 us -> 27.2 us
  local copies, waits for them, and re-layouts: 32.5 us -> 27.2 us
  matrix products: 37.7 us -> 34.4 us
    all_gather x3 -> x1, waiting for transfers between devices: 104 us -> 59 us  [denoise(): lax.all_gather(jnp.concatenate([wq, wk, wv], axis=1), 'tile', axis=0, til...]
    dot_general x3 -> x0, local copies, waits for them, and re-layouts: 19.5 us -> none  [add_rows(): return jnp.dot(left, shard_rows, preferred_element_type=jnp.float32)]
    unnamed x25 -> x36, local copies, waits for them, and re-layouts: 5.88 us -> 19.5 us
    all_gather x1, waiting for transfers between devices: 19.2 us -> 10.3 us  [denoise(): lax.all_gather(wo, 'tile', axis=1, tiled=True)]
    dot_general x1, matrix products: 10.3 us -> 2.02 us  [denoise(): jnp.einsum('nhqk,nkhd->nqhd', probs, value_half, preferred_element_type=j...]
    dot_general x2 -> x1, matrix products: 10.1 us -> 13.5 us  [add_rows(): return jnp.dot(left, shard_rows, preferred_element_type=jnp.float32)]
    reduce_sum x2, other arithmetic: 1.51 us -> 4.54 us  [layer_norm(): spread = jnp.mean(center * center, axis=-1, keepdims=True)]
    convert_element_type x1, other arithmetic: 2.83 us -> 5.56 us  [denoise(): (layer_norm(hidden0) * (1.0 + scale_vec) + shift_vec).astype(jnp.bfloat16)]
  transfers between devices with their start and end apart: 6 -> 4, of which waited for: 5 -> 3; matrix products, arithmetic and copies ran while one was open for 23% -> 28% of each run, Pallas kernels for 0% -> 0%
where the time goes in v1:
time: 206 us
  waiting for transfers between devices  72.9 us (35%)
  matrix products  34.4 us (17%)
  local copies, waits for them, and re-layouts  27.2 us (13%)
  other arithmetic  27.2 us (13%)
  blocking collectives  23.4 us (11%)
  between operations  15.5 us (8%)
  starting transfers between devices  5.17 us (3%)
    all_gather x1, waiting for transfers between devices, denoise(): lax.all_gather(jnp.concatenate([wq, wk, wv], axis=1), 'tile', axis=0, til...  59 us
    all_gather x1, blocking collectives, on_device(): modulation = lax.all_gather(local_mod, 'tile', axis=1, tiled=True)  23.4 us
    unnamed x36, local copies, waits for them, and re-layouts  19.5 us
    dot_general x1, matrix products, add_rows(): return jnp.dot(left, shard_rows, preferred_element_type=jnp.float32)  13.5 us
    all_gather x1, waiting for transfers between devices, denoise(): lax.all_gather(wo, 'tile', axis=1, tiled=True)  10.3 us
    dot_general x1, matrix products, denoise(): jnp.dot(mixed, lax.all_gather(wo, 'tile', axis=1, tiled=True), preferred_...  7.19 us
    dot_general x9, matrix products, on_device(): jnp.einsum('oc,chw->ohw', conv_w[3 * row_shift + col_shift], window, prec...  5.81 us
    convert_element_type x1, other arithmetic, denoise(): (layer_norm(hidden0) * (1.0 + scale_vec) + shift_vec).astype(jnp.bfloat16)  5.56 us
  transfers between devices with their start and end apart: 4, of which 3 were waited for; matrix products, arithmetic and copies ran while one was open for 28% of the time, Pallas kernels for 0%

profile of v1, /device:TPU:1, one launch (start us, length us, event | category | flops | bytes accessed | tf_op | source)
XLA Modules:
  0.0 205.7 jit_solution(2429760494981325304)
XLA Ops:
  7.2 2.1 %pad_maximum_fusion = bf16[128,3072]{1,0:T(8,128)(2,1)} fusion(bf16[128,1024]{1,0:T(8,128)(2,1)} %param.26, bf16[128,1024]{1,0:T(8,128)(2,1)} %param.25, bf16[128,1024]{1,0:T(8,128)(2,1)} %param.24), kind=kLoop, calls=%fused_computation.64 | loop fusion | flops 2359296 | bytes 1572864 | tf_op jit(solution)/shard_map/concatenate | solution.py:102
  12.6 1.5 copy.83
  14.2 1.1 copy.84
  15.8 1.5 convert_element_type.55
  17.9 3.7 %fusion.83 = (f32[3,256]{1,0:T(4,128)S(1)}, f32[3,256,2048]{2,1,0:T(8,128)}) fusion(f32[256,2048]{1,0:T(8,128)S(1)} %convert_element_type.55, bf16[128,2048]{1,0:T(8,128)(2,1)S(1)} %copy-done, bf16[3,256,128]{2,1,0:T(8,128)(2,1)S(1)} %gather_fusion, pred[3]{0:T(512)(128)(4,1)S(1)} %compare_and_fusion), kind=kOutput, calls=%fused_computation.142 | convolution fusion | flops 405896448 | bytes 9112579 | tf_op jit(solution)/shard_map/dot_general | solution.py:92
  21.6 3.8 %multiply_reduce_fusion.1 = f32[3,256]{1,0:T(4,128)S(1)} fusion(f32[3,256,2048]{2,1,0:T(8,128)} %get-tuple-element.26, f32[3,256]{1,0:T(4,128)S(1)} %broadcast_multiply_fusion.1), kind=kLoop, calls=%fused_computation.13 | loop fusion | flops 4717824 | bytes 6297600 | tf_op jit(solution)/shard_map/reduce_sum | solution.py:43
  25.6 23.4 %all-gather.1 = f32[16,1,384]{2,1,0:T(1,128)S(1)} all-gather(f32[1,1,384]{2,1,0:T(1,128)S(1)} %convolution_bitcast_fusion), channel_id=2, replica_groups=mesh['grp'=2,'tile'=16] {'tile'}, dimensions={0}, use_global_device_ids=true | all-gather | bytes 26112 | tf_op jit(solution)/shard_map/all_gather | solution.py:154
  49.2 5.6 %fusion.4 = bf16[768,2048]{1,0:T(8,128)(2,1)} fusion(f32[3,256,2048]{2,1,0:T(8,128)} %get-tuple-element.26, f32[2048]{0:T(1024)S(1)} %bitcast.139, f32[2048]{0:T(1024)S(1)} %bitcast.138, f32[768]{0:T(1024)S(1)} %rsqrt.36, f32[768]{0:T(1024)S(1)} %div.60), kind=kLoop, calls=%fused_computation.8 | loop fusion | flops 7864320 | bytes 9459712 | tf_op jit(solution)/shard_map/convert_element_type | solution.py:96
  54.7 59.0 %all-gather.5.cloned.1.call-done = bf16[2048,3072]{1,0:T(8,128)(2,1)} async-done(((bf16[128,3072]{1,0:T(8,128)(2,1)}), bf16[2048,3072]{1,0:T(8,128)(2,1)}) %all-gather.5.cloned.1.call-update) | async-done | bytes 12582928 | tf_op jit(solution)/shard_map/all_gather | solution.py:102
  113.7 13.5 %fusion.86 = f32[768,3072]{1,0:T(8,128)S(1)} fusion(bf16[768,2048]{1,0:T(8,128)(2,1)} %fusion.4, bf16[2048,3072]{1,0:T(8,128)(2,1)} %all-gather.5.cloned.1.call-done), kind=kOutput, calls=%fused_computation.145 | convolution fusion | flops 9663676416 | bytes 25165824 | tf_op jit(solution)/shard_map/dot_general | solution.py:71
  127.2 2.8 %slice_bitcast_fusion.1 = (f32[96,8,8,128]{3,1,2,0:T(8,128)S(1)}, f32[96,8,8,128]{3,1,2,0:T(8,128)}) fusion(f32[768,3072]{1,0:T(8,128)S(1)} %fusion.86), kind=kLoop, calls=%fused_computation.29 | loop fusion | bytes 12582912
  130.0 1.9 copy-done.6
  132.6 1.6 copy-done.2
  135.5 2.6 %copy.104 = f32[96,8,8,128]{3,2,1,0:T(8,128)S(1)} copy(f32[96,8,8,128]{3,1,2,0:T(8,128)} %get-tuple-element.18) | data formatting | bytes 6291456
  138.1 1.7 copy-done.4
  141.0 2.8 %fusion.20 = bf16[96,8,8,128]{3,1,2,0:T(8,128)(2,1)S(1)} fusion(f32[768,3072]{1,0:T(8,128)} %copy-done.6), kind=kLoop, calls=%fused_computation.41 | loop fusion | bytes 3145728
  144.3 1.0 fusion.14
  146.2 1.0 fusion.11
  148.2 4.8 %fusion.84 = (f32[3,8,256]{2,1,0:T(8,128)S(1)}, f32[3,8,256,256]{2,3,1,0:T(8,128)S(1)}) fusion(f32[3,8,256,256]{2,3,1,0:T(8,128)S(1)} %fusion.24), kind=kOutput, calls=%fused_computation.143 | output fusion | flops 6291711 | bytes 12607488 | tf_op jit(solution)/shard_map/sub | solution.py:114
  153.0 2.0 fusion.27
  155.0 2.0 copy.93
  157.0 10.3 %all-gather.7.cloned.1.call-done = bf16[1024,2048]{1,0:T(8,128)(2,1)} async-done(((bf16[1024,128]{1,0:T(8,128)(2,1)}), bf16[1024,2048]{1,0:T(8,128)(2,1)}) %all-gather.7.cloned.1.call-update) | async-done | bytes 4194320 | tf_op jit(solution)/shard_map/all_gather | solution.py:119
  167.3 7.2 %fusion.85 = (f32[768]{0:T(1024)S(1)}, f32[768,2048]{1,0:T(8,128)S(1)}) fusion(bf16[1024,2048]{1,0:T(8,128)(2,1)} %all-gather.7.cloned.1.call-done, bf16[96,8,8,128]{3,2,1,0:T(8,128)(2,1)S(1)} %bitcast.135, f32[2048]{0:T(1024)S(1)} %bitcast.140, f32[3,256,2048]{2,1,0:T(8,128)} %get-tuple-element.26), kind=kOutput, calls=%fused_computation.144 | convolution fusion | flops 3225943296 | bytes 18361344 | tf_op jit(solution)/shard_map/dot_general | solution.py:118
  175.6 1.1 fusion.33
  177.7 1.1 multiply_bitcast_fusion
  178.8 1.1 copy.94
  180.5 1.6 copy_select_fusion
  182.2 3.2 %collective-permute-start = (f32[32,1,128]{2,0,1:T(8,128)S(1)}, f32[32,1,128]{2,0,1:T(8,128)S(1)}, u32[]{:S(2)}, u32[]{:S(2)}) collective-permute-start(f32[32,1,128]{2,0,1:T(8,128)S(1)} %get-tuple-element.19), channel_id=1, source_target_pairs={{0,1},{1,2},{2,3},{3,4},{4,5},{5,6},{6,7},{7,8},{8,9},{9,10},{10,1... | collective-permute-start | bytes 49160 | tf_op jit(solution)/shard_map/ppermute | solution.py:20
  185.3 1.9 collective-permute-start.1
  187.5 2.9 %collective-permute-done.1 = f32[32,1,128]{2,0,1:T(8,128)S(1)} collective-permute-done((f32[32,1,128]{2,0,1:T(8,128)S(1)}, f32[32,1,128]{2,0,1:T(8,128)S(1)}, u32[]{:S(2)}, u32[]{:S(2)}) %collective-permute-start.1) | collective-permute-done | bytes 16416 | tf_op jit(solution)/shard_map/ppermute | solution.py:23
  196.7 1.1 copy.100
  197.8 1.1 copy.99
  (81 shorter events, 18.3 us)
Async XLA Ops:
  7.2 10.7 %copy-start = (bf16[128,2048]{1,0:T(8,128)(2,1)S(1)}, bf16[128,2048]{1,0:T(8,128)(2,1)}, u32[]{:S(2)}) copy-start(bf16[128,2048]{1,0:T(8,128)(2,1)} %param.22) | copy-start | bytes 1572868
  7.2 106.6 %all-gather.5.cloned.1.call-start = ((), (), s32[]{:S(2)}) async-start(), calls=%async_computation | async-start | bytes 13369344 | tf_op jit(solution)/shard_map/all_gather | solution.py:102
  9.4 158.0 %all-gather.7.cloned.1.call-start = ((), (), s32[]{:S(2)}) async-start(), calls=%async_computation.1 | async-start | bytes 4456448 | tf_op jit(solution)/shard_map/all_gather | solution.py:119
  21.6 3.9 %copy-start.10 = (bf16[256,384]{1,0:T(8,128)(2,1)S(1)}, bf16[256,384]{1,0:T(8,128)(2,1)}, u32[]{:S(2)}) copy-start(bf16[256,384]{1,0:T(8,128)(2,1)} %param.23) | copy-start | bytes 589828
  127.2 4.7 %copy-start.6 = (f32[768,3072]{1,0:T(8,128)}, f32[768,3072]{1,0:T(8,128)S(1)}, u32[]{:S(2)}) copy-start(f32[768,3072]{1,0:T(8,128)S(1)} %fusion.86) | copy-start | bytes 28311556
  132.6 1.6 copy-start.2
  138.1 1.7 copy-start.4
  141.0 3.3 %copy-start.3 = (f32[96,8,8,128]{3,2,1,0:T(8,128)S(1)}, f32[96,8,8,128]{3,2,1,0:T(8,128)}, u32[]{:S(2)}) copy-start(f32[96,8,8,128]{3,2,1,0:T(8,128)} %copy-done.2) | copy-start | bytes 9437188
  141.0 3.3 %copy-start.12 = (f32[128]{0:T(128)S(1)}, f32[128]{0:T(128)}, u32[]{:S(2)}) copy-start(f32[128]{0:T(128)} %param.28) | copy-start | bytes 1540
  144.2 1.9 copy-start.5
  144.2 1.9 copy-start.13
  174.5 1.0 copy-start.9
  178.7 1.8 copy-start.7
  179.9 10.8 %copy-start.11 = (f32[9,32,32]{2,1,0:T(8,128)S(1)}, f32[9,32,32]{2,1,0:T(8,128)}, u32[]{:S(2)}) copy-start(f32[9,32,32]{2,1,0:T(8,128)} %param.31) | copy-start | bytes 110596
  182.2 5.3 %collective-permute-start = (f32[32,1,128]{2,0,1:T(8,128)S(1)}, f32[32,1,128]{2,0,1:T(8,128)S(1)}, u32[]{:S(2)}, u32[]{:S(2)}) collective-permute-start(f32[32,1,128]{2,0,1:T(8,128)S(1)} %get-tuple-element.19), channel_id=1, source_target_pairs={{0,1},{1,2},{2,3},{3,4},{4,5},{5,6},{6,7},{7,8},{8,9},{9,10},{10,1... | collective-permute-start | bytes 49160 | tf_op jit(solution)/shard_map/ppermute | solution.py:20
  185.3 5.1 %collective-permute-start.1 = (f32[32,1,128]{2,0,1:T(8,128)S(1)}, f32[32,1,128]{2,0,1:T(8,128)S(1)}, u32[]{:S(2)}, u32[]{:S(2)}) collective-permute-start(f32[32,1,128]{2,0,1:T(8,128)S(1)} %get-tuple-element.20), channel_id=1, source_target_pairs={{1,0},{2,1},{3,2},{4,3},{5,4},{6,5},{7,6},{8,7},{9,8},{10,9},{11,1... | collective-permute-start | bytes 49160 | tf_op jit(solution)/shard_map/ppermute | solution.py:23
  193.3 2.5 %copy-start.8 = (f32[32,32,128]{2,1,0:T(8,128)S(1)}, f32[32,32,128]{2,1,0:T(8,128)}, u32[]{:S(2)}) copy-start(f32[32,32,128]{2,1,0:T(8,128)} %param.18) | copy-start | bytes 1572868
  195.2 3.7 %copy-start.1 = (bf16[128,2048]{1,0:T(8,128)(2,1)S(1)}, bf16[128,2048]{1,0:T(8,128)(2,1)}, u32[]{:S(2)}) copy-start(bf16[128,2048]{1,0:T(8,128)(2,1)} %param.22) | copy-start | bytes 1572868
Sparse Core Ops, SparseCore 0:
  10.3 103.3 all-gather.4
  115.9 51.3 all-gather.6

commit v2 on v1

--- a/solution.py
+++ b/solution.py
@@ -65,6 +65,13 @@
     return jnp.transpose(shaped, (5, 1, 3, 0, 2, 4)).reshape(
         channels, tile_side * PATCH, tiles_here * tile_side * PATCH
     )
+
+
+def spread_columns(w_local):
+    count = lax.axis_size("tile")
+    copies = jnp.broadcast_to(w_local[None], (count,) + w_local.shape)
+    got = lax.all_to_all(copies, "tile", 0, 0, tiled=True)
+    return jnp.transpose(got, (1, 0, 2)).reshape(w_local.shape[0], -1)
 
 
 def add_rows(left, shard_rows):
@@ -115,9 +122,7 @@
     probs = (expo / jnp.sum(expo, axis=-1, keepdims=True)).astype(jnp.bfloat16)
     mixed = jnp.einsum("nhqk,nkhd->nqhd", probs, value_half, preferred_element_type=jnp.float32)
     mixed = mixed.astype(jnp.bfloat16).reshape(row_count, -1)
-    attn_out = jnp.dot(
-        mixed, lax.all_gather(wo, "tile", axis=1, tiled=True), preferred_element_type=jnp.float32
-    )
+    attn_out = jnp.dot(mixed, spread_columns(wo), preferred_element_type=jnp.float32)
     hidden1 = hidden0 + gate_vec * attn_out
     final = layer_norm(hidden1).astype(jnp.bfloat16)
     eps_pred = jnp.dot(final, out_w, preferred_element_type=jnp.float32).astype(jnp.bfloat16)

time: 206 us -> 287 us (1.39)
  blocking collectives: 23.4 us -> 98 us
  starting transfers between devices: 5.17 us -> 23.3 us
  waiting for transfers between devices: 72.9 us -> 56.5 us
    all_gather x1, blocking collectives: 23.4 us -> 98 us  [on_device(): modulation = lax.all_gather(local_mod, 'tile', axis=1, tiled=True)]
    ppermute x1, starting transfers between devices: 3.17 us -> 13.9 us  [padded_2(): lax.ppermute(lax.slice_in_dim(block, block.shape[dim] - width, None, axis...]
    all_gather x1 -> x0, waiting for transfers between devices: 10.3 us -> none  [denoise(): lax.all_gather(wo, 'tile', axis=1, tiled=True)]
    all_to_all x0 -> x1, starting transfers between devices: none -> 7.48 us  [spread_columns(): got = lax.all_to_all(copies, 'tile', 0, 0, tiled=True)]
    all_gather x1, waiting for transfers between devices: 59 us -> 53.6 us  [denoise(): lax.all_gather(jnp.concatenate([wq, wk, wv], axis=1), 'tile', axis=0, til...]
    unnamed x36 -> x39, local copies, waits for them, and re-layouts: 19.5 us -> 19 us
  transfers between devices with their start and end apart: 4 -> 4, of which waited for: 3 -> 2; matrix products, arithmetic and copies ran while one was open for 28% -> 21% of each run, Pallas kernels for 0% -> 0%
where the time goes in v2:
time: 287 us; the launch traced here: 284 us
  blocking collectives  98 us (34%)
  waiting for transfers between devices  56.5 us (20%)
  matrix products  35.3 us (12%)
  local copies, waits for them, and re-layouts  29.9 us (10%)
  other arithmetic  25.8 us (9%)
  starting transfers between devices  23.3 us (8%)
  between operations  15.5 us (5%)
    all_gather x1, blocking collectives, on_device(): modulation = lax.all_gather(local_mod, 'tile', axis=1, tiled=True)  98 us
    all_gather x1, waiting for transfers between devices, denoise(): lax.all_gather(jnp.concatenate([wq, wk, wv], axis=1), 'tile', axis=0, til...  53.6 us
    unnamed x39, local copies, waits for them, and re-layouts  19 us
    ppermute x1, starting transfers between devices, padded_2(): lax.ppermute(lax.slice_in_dim(block, block.shape[dim] - width, None, axis...  13.9 us
    dot_general x1, matrix products, add_rows(): return jnp.dot(left, shard_rows, preferred_element_type=jnp.float32)  13.5 us
    all_to_all x1, starting transfers between devices, spread_columns(): got = lax.all_to_all(copies, 'tile', 0, 0, tiled=True)  7.48 us
    dot_general x1, matrix products, denoise(): jnp.dot(mixed, spread_columns(wo), preferred_element_type=jnp.float32)  7.26 us
    dot_general x9, matrix products, on_device(): jnp.einsum('oc,chw->ohw', conv_w[3 * row_shift + col_shift], window, prec...  5.81 us
  transfers between devices with their start and end apart: 4, of which 2 were waited for; matrix products, arithmetic and copies ran while one was open for 21% of the time, Pallas kernels for 0%

profile of v2, /device:TPU:1, one launch (start us, length us, event | category | flops | bytes accessed | tf_op | source)
XLA Modules:
  0.0 284.2 jit_solution(10598820612288547545)
XLA Ops:
  7.2 2.1 pad_maximum_fusion
  9.4 1.1 copy.98
  10.4 2.6 broadcast_in_dim.100
  13.0 7.5 %all-to-all-start = ((bf16[16,1024,128]{1,2,0:T(8,128)(2,1)}), bf16[16,1024,128]{1,2,0:T(8,128)(2,1)}, u32[]{:S(2)}, u32[]{:S(2)}) async-start(bf16[16,1024,128]{1,2,0:T(8,128)(2,1)} %broadcast_in_dim.100), calls=%async_computation | async-start | bytes 8388608 | tf_op jit(solution)/shard_map/all_to_all | solution.py:73
  21.8 1.1 copy.88
  23.5 1.5 convert_element_type.55
  25.3 1.3 gather_fusion
  26.6 4.5 %fusion.83 = (f32[3,256]{1,0:T(4,128)S(1)}, f32[3,256,2048]{2,1,0:T(8,128)}) fusion(f32[256,2048]{1,0:T(8,128)S(1)} %convert_element_type.55, bf16[128,2048]{1,0:T(8,128)(2,1)S(1)} %copy-done, bf16[3,256,128]{2,1,0:T(8,128)(2,1)} %gather_fusion, pred[3]{0:T(512)(128)(4,1)S(1)} %compare_and_fusion), kind=kOutput, calls=%fused_computation.142 | convolution fusion | flops 405896448 | bytes 9112579 | tf_op jit(solution)/shard_map/dot_general | solution.py:99
  31.1 3.6 %multiply_reduce_fusion.1 = f32[3,256]{1,0:T(4,128)S(1)} fusion(f32[3,256,2048]{2,1,0:T(8,128)} %get-tuple-element.26, f32[3,256]{1,0:T(4,128)S(1)} %broadcast_multiply_fusion.1), kind=kLoop, calls=%fused_computation.13 | loop fusion | flops 4717824 | bytes 6297600 | tf_op jit(solution)/shard_map/reduce_sum | solution.py:43
  35.2 98.0 %all-gather.1 = f32[16,1,384]{2,1,0:T(1,128)S(1)} all-gather(f32[1,1,384]{2,1,0:T(1,128)S(1)} %convolution_bitcast_fusion), channel_id=2, replica_groups=mesh['grp'=2,'tile'=16] {'tile'}, dimensions={0}, use_global_device_ids=true | all-gather | bytes 26112 | tf_op jit(solution)/shard_map/all_gather | solution.py:159
  133.2 5.6 %fusion.4 = bf16[768,2048]{1,0:T(8,128)(2,1)} fusion(f32[3,256,2048]{2,1,0:T(8,128)} %get-tuple-element.26, f32[2048]{0:T(1024)S(1)} %bitcast.142, f32[2048]{0:T(1024)S(1)} %bitcast.141, f32[768]{0:T(1024)S(1)} %rsqrt.36, f32[768]{0:T(1024)S(1)} %div.60), kind=kLoop, calls=%fused_computation.8 | loop fusion | flops 7864320 | bytes 9459712 | tf_op jit(solution)/shard_map/convert_element_type | solution.py:103
  138.8 53.6 %all-gather.4.cloned.1.call-done = bf16[2048,3072]{1,0:T(8,128)(2,1)} async-done(((bf16[128,3072]{1,0:T(8,128)(2,1)}), bf16[2048,3072]{1,0:T(8,128)(2,1)}) %all-gather.4.cloned.1.call-update) | async-done | bytes 12582928 | tf_op jit(solution)/shard_map/all_gather | solution.py:109
  192.3 13.5 %fusion.86 = f32[768,3072]{1,0:T(8,128)S(1)} fusion(bf16[768,2048]{1,0:T(8,128)(2,1)} %fusion.4, bf16[2048,3072]{1,0:T(8,128)(2,1)} %all-gather.4.cloned.1.call-done), kind=kOutput, calls=%fused_computation.145 | convolution fusion | flops 9663676416 | bytes 25165824 | tf_op jit(solution)/shard_map/dot_general | solution.py:78
  205.8 2.8 slice_bitcast_fusion.1
  208.6 1.7 copy-done.6
  211.1 1.6 copy-done.2
  213.9 2.6 copy.109
  216.5 1.7 copy-done.4
  219.5 2.4 fusion.20
  222.4 1.0 fusion.14
  226.3 4.8 %fusion.84 = (f32[3,8,256]{2,1,0:T(8,128)S(1)}, f32[3,8,256,256]{2,3,1,0:T(8,128)S(1)}) fusion(f32[3,8,256,256]{2,3,1,0:T(8,128)S(1)} %fusion.24), kind=kOutput, calls=%fused_computation.143 | output fusion | flops 6291711 | bytes 12607488 | tf_op jit(solution)/shard_map/sub | solution.py:121
  231.1 2.0 fusion.27
  233.1 2.0 copy.97
  235.1 7.3 %fusion.85 = (f32[768]{0:T(1024)S(1)}, f32[768,2048]{1,0:T(8,128)S(1)}) fusion(bf16[1024,2048]{0,1:T(8,128)(2,1)} %bitcast.15, bf16[96,8,8,128]{3,2,1,0:T(8,128)(2,1)S(1)} %bitcast.138, f32[2048]{0:T(1024)S(1)} %bitcast.143, f32[3,256,2048]{2,1,0:T(8,128)} %get-tuple-element.26), kind=kOutput, calls=%fused_computation.144 | convolution fusion | flops 3225943296 | bytes 18361344 | tf_op jit(solution)/shard_map/dot_general | solution.py:125
  245.5 1.1 multiply_bitcast_fusion
  246.6 1.1 copy.99
  248.3 1.6 copy_select_fusion
  249.9 13.9 %collective-permute-start = (f32[32,1,128]{2,0,1:T(8,128)S(1)}, f32[32,1,128]{2,0,1:T(8,128)S(1)}, u32[]{:S(2)}, u32[]{:S(2)}) collective-permute-start(f32[32,1,128]{2,0,1:T(8,128)S(1)} %get-tuple-element.19), channel_id=1, source_target_pairs={{0,1},{1,2},{2,3},{3,4},{4,5},{5,6},{6,7},{7,8},{8,9},{9,10},{10,1... | collective-permute-start | bytes 49160 | tf_op jit(solution)/shard_map/ppermute | solution.py:20
  263.8 1.9 collective-permute-start.1
  266.0 2.9 %collective-permute-done.1 = f32[32,1,128]{2,0,1:T(8,128)S(1)} collective-permute-done((f32[32,1,128]{2,0,1:T(8,128)S(1)}, f32[32,1,128]{2,0,1:T(8,128)S(1)}, u32[]{:S(2)}, u32[]{:S(2)}) %collective-permute-start.1) | collective-permute-done | bytes 16416 | tf_op jit(solution)/shard_map/ppermute | solution.py:23
  275.2 1.1 copy.104
  276.3 1.1 copy.105
  (84 shorter events, 18.2 us)
Async XLA Ops:
  7.2 19.4 %copy-start = (bf16[128,2048]{1,0:T(8,128)(2,1)S(1)}, bf16[128,2048]{1,0:T(8,128)(2,1)}, u32[]{:S(2)}) copy-start(bf16[128,2048]{1,0:T(8,128)(2,1)} %param.22) | copy-start | bytes 1572868
  7.2 185.2 %all-gather.4.cloned.1.call-start = ((), (), s32[]{:S(2)}) async-start(), calls=%async_computation.1 | async-start | bytes 13369344 | tf_op jit(solution)/shard_map/all_gather | solution.py:109
  13.0 8.3 %copy-start.7 = (f32[32,32,128]{2,1,0:T(8,128)S(1)}, f32[32,32,128]{2,1,0:T(8,128)}, u32[]{:S(2)}) copy-start(f32[32,32,128]{2,1,0:T(8,128)} %param.16) | copy-start | bytes 1572868
  13.0 222.1 %all-to-all-start = ((bf16[16,1024,128]{1,2,0:T(8,128)(2,1)}), bf16[16,1024,128]{1,2,0:T(8,128)(2,1)}, u32[]{:S(2)}, u32[]{:S(2)}) async-start(bf16[16,1024,128]{1,2,0:T(8,128)(2,1)} %broadcast_in_dim.100), calls=%async_computation | async-start | bytes 8388608 | tf_op jit(solution)/shard_map/all_to_all | solution.py:73
  21.8 3.1 %copy-start.12 = (s32[4]{0:T(128)S(1)}, s32[4]{0:T(128)}, u32[]{:S(2)}) copy-start(s32[4]{0:T(128)} %param.19) | copy-start | bytes 52
  31.1 3.9 %copy-start.10 = (bf16[256,384]{1,0:T(8,128)(2,1)S(1)}, bf16[256,384]{1,0:T(8,128)(2,1)}, u32[]{:S(2)}) copy-start(bf16[256,384]{1,0:T(8,128)(2,1)} %param.23) | copy-start | bytes 589828
  205.8 4.5 %copy-start.6 = (f32[768,3072]{1,0:T(8,128)}, f32[768,3072]{1,0:T(8,128)S(1)}, u32[]{:S(2)}) copy-start(f32[768,3072]{1,0:T(8,128)S(1)} %fusion.86) | copy-start | bytes 28311556
  211.1 1.6 copy-start.2
  216.5 1.7 copy-start.4
  219.5 2.9 %copy-start.3 = (f32[96,8,8,128]{3,2,1,0:T(8,128)S(1)}, f32[96,8,8,128]{3,2,1,0:T(8,128)}, u32[]{:S(2)}) copy-start(f32[96,8,8,128]{3,2,1,0:T(8,128)} %copy-done.2) | copy-start | bytes 9437188
  219.5 2.9 %copy-start.13 = (f32[128]{0:T(128)S(1)}, f32[128]{0:T(128)}, u32[]{:S(2)}) copy-start(f32[128]{0:T(128)} %param.28) | copy-start | bytes 1540
  222.3 1.9 copy-start.5
  222.4 1.9 copy-start.14
  242.4 1.0 copy-start.9
  247.7 21.5 %copy-start.11 = (f32[9,32,32]{2,1,0:T(8,128)S(1)}, f32[9,32,32]{2,1,0:T(8,128)}, u32[]{:S(2)}) copy-start(f32[9,32,32]{2,1,0:T(8,128)} %param.31) | copy-start | bytes 110596
  249.9 16.1 %collective-permute-start = (f32[32,1,128]{2,0,1:T(8,128)S(1)}, f32[32,1,128]{2,0,1:T(8,128)S(1)}, u32[]{:S(2)}, u32[]{:S(2)}) collective-permute-start(f32[32,1,128]{2,0,1:T(8,128)S(1)} %get-tuple-element.19), channel_id=1, source_target_pairs={{0,1},{1,2},{2,3},{3,4},{4,5},{5,6},{6,7},{7,8},{8,9},{9,10},{10,1... | collective-permute-start | bytes 49160 | tf_op jit(solution)/shard_map/ppermute | solution.py:20
  263.8 5.1 %collective-permute-start.1 = (f32[32,1,128]{2,0,1:T(8,128)S(1)}, f32[32,1,128]{2,0,1:T(8,128)S(1)}, u32[]{:S(2)}, u32[]{:S(2)}) collective-permute-start(f32[32,1,128]{2,0,1:T(8,128)S(1)} %get-tuple-element.20), channel_id=1, source_target_pairs={{1,0},{2,1},{3,2},{4,3},{5,4},{6,5},{7,6},{8,7},{9,8},{10,9},{11,1... | collective-permute-start | bytes 49160 | tf_op jit(solution)/shard_map/ppermute | solution.py:23
  271.8 2.5 copy-start.8
  273.7 3.7 %copy-start.1 = (bf16[128,2048]{1,0:T(8,128)(2,1)S(1)}, bf16[128,2048]{1,0:T(8,128)(2,1)}, u32[]{:S(2)}) copy-start(bf16[128,2048]{1,0:T(8,128)(2,1)} %param.22) | copy-start | bytes 1572868
Sparse Core Ops, SparseCore 0:
  10.3 181.9 all-gather.3

commit v3 on v1

--- a/solution.py
+++ b/solution.py
@@ -10,19 +10,6 @@
 MAXOWN = 3
 TSTEPS = 1000
 STRIDE = 20
-
-
-def padded_2(block, sides, width):
-    for axis, dim in sides:
-        count = lax.axis_size(axis)
-        forward = [(i, i + 1) for i in range(count - 1)]
-        backward = [(target, source) for source, target in forward]
-        low = lax.ppermute(
-            lax.slice_in_dim(block, block.shape[dim] - width, None, axis=dim), axis, forward
-        )
-        high = lax.ppermute(lax.slice_in_dim(block, 0, width, axis=dim), axis, backward)
-        block = jnp.concatenate([low, block, high], axis=dim)
-    return block
 
 
 def plan(step):
@@ -122,6 +109,53 @@
     final = layer_norm(hidden1).astype(jnp.bfloat16)
     eps_pred = jnp.dot(final, out_w, preferred_element_type=jnp.float32).astype(jnp.bfloat16)
     return eps_pred.reshape(count, tokens_tile, token_values)
+
+
+def taps(conv_w, window, a, b):
+    return jnp.einsum(
+        "oc,c...->o...", conv_w[3 * a + b], window, precision=lax.Precision.HIGHEST
+    )
+
+
+def seam_blend(raw, conv_w, tile_px):
+    channels, rows, cols = raw.shape
+    count = lax.axis_size("tile")
+    forward = [(i, i + 1) for i in range(count - 1)]
+    backward = [(target, source) for source, target in forward]
+    low = lax.ppermute(raw[:, rows - 1 :], "tile", forward)
+    high = lax.ppermute(raw[:, :1], "tile", backward)
+
+    seam_cols = [j for j in range(cols) if j % tile_px in (0, tile_px - 1)]
+    framed = jnp.pad(raw, ((0, 0), (1, 1), (1, 1)))
+    shifted = [jnp.stack([framed[:, :, j + b] for j in seam_cols], axis=-1) for b in range(3)]
+    by_col = None
+    for a in range(3):
+        for b in range(3):
+            term = taps(conv_w, shifted[b][:, a : a + rows], a, b)
+            by_col = term if by_col is None else by_col + term
+
+    edge = jnp.concatenate([low, raw[:, :2], raw[:, rows - 2 :], high], axis=1)
+    edge = jnp.pad(edge, ((0, 0), (0, 0), (1, 1)))
+    by_row = None
+    for a in range(3):
+        for b in range(3):
+            window = jnp.stack([edge[:, a, b : b + cols], edge[:, 3 + a, b : b + cols]], axis=1)
+            term = taps(conv_w, window, a, b)
+            by_row = term if by_row is None else by_row + term
+
+    pieces = []
+    done = 0
+    for k, j in enumerate(seam_cols):
+        if j > done:
+            pieces.append(raw[:, :, done:j])
+        pieces.append(by_col[:, :, k : k + 1])
+        done = j + 1
+    if done < cols:
+        pieces.append(raw[:, :, done:])
+    mixed_cols = jnp.concatenate(pieces, axis=2)
+    return jnp.concatenate(
+        [by_row[:, :1], mixed_cols[:, 1 : rows - 1], by_row[:, 1:]], axis=1
+    )
 
 
 def on_device(
@@ -185,24 +219,7 @@
     raw_estimate = jnp.where(
         cloud_cols[None, None, :], (latent - sin_now * eps_latent) / cos_now, observed
     )
-    padded = padded_2(raw_estimate, (("tile", 1),), 1)
-    padded = jnp.pad(padded, ((0, 0), (0, 0), (1, 1)))
-    blended = jnp.zeros_like(raw_estimate)
-    for row_shift in range(3):
-        for col_shift in range(3):
-            window = padded[:, row_shift : row_shift + band_rows, col_shift : col_shift + band_cols]
-            blended = blended + jnp.einsum(
-                "oc,chw->ohw",
-                conv_w[3 * row_shift + col_shift],
-                window,
-                precision=lax.Precision.HIGHEST,
-            )
-    row_pos = jnp.arange(band_rows) % band_rows
-    col_pos = jnp.arange(band_cols) % band_rows
-    seam_mask = ((row_pos == 0) | (row_pos == band_rows - 1))[:, None] | (
-        (col_pos == 0) | (col_pos == band_rows - 1)
-    )[None, :]
-    estimate = jnp.where(seam_mask[None], blended, raw_estimate)
+    estimate = seam_blend(raw_estimate, conv_w, band_rows)
     next_latent = cos_prev * estimate + sin_prev * noise
     return (estimate, next_latent)
 

time: 206 us -> 241 us (1.17)
  local copies, waits for them, and re-layouts: 27.2 us -> 59.2 us
  waiting for transfers between devices: 72.9 us -> 69.9 us
  other arithmetic: 27.2 us -> 30 us
    slice x1 -> x28, local copies, waits for them, and re-layouts: 0.01 us -> 20.8 us  [the longest x12 11 us: seam_blend(): term = taps(conv_w, shifted[b][:, a:a + rows], a, b)]
    another operation x0 -> x3, local copies, waits for them, and re-layouts: none -> 5.79 us  [seam_blend(): jnp.stack([framed[:, :, j + b] for j in seam_cols], axis=-1)]
    concatenate x0 -> x1, local copies, waits for them, and re-layouts: none -> 4.56 us  [seam_blend(): mixed_cols = jnp.concatenate(pieces, axis=2)]
    add x0 -> x2, other arithmetic: none -> 3.02 us  [the longest x1 1.65 us: seam_blend(): by_col = term if by_col is None else by_col + term]
    ppermute x2, waiting for transfers between devices: 2.88 us -> 0.01 us  [the longest x1 0.01 us: seam_blend(): high = lax.ppermute(raw[:, :1], 'tile', backward)]
    dot_general x9 -> x18, matrix products: 5.81 us -> 7.66 us  [taps(): jnp.einsum('oc,c...->o...', conv_w[3 * a + b], window, precision=lax.Prec...]
    unnamed x36 -> x48, local copies, waits for them, and re-layouts: 19.5 us -> 19.5 us
  transfers between devices with their start and end apart: 4 -> 4, of which waited for: 3 -> 2; matrix products, arithmetic and copies ran while one was open for 28% -> 27% of each run, Pallas kernels for 0% -> 0%
where the time goes in v3:
time: 241 us; the launch traced here: 240 us
  waiting for transfers between devices  69.9 us (29%)
  local copies, waits for them, and re-layouts  59.2 us (25%)
  matrix products  36.2 us (15%)
  other arithmetic  30 us (12%)
  blocking collectives  23.3 us (10%)
  between operations  15.7 us (7%)
  starting transfers between devices  5.42 us (2%)
    all_gather x1, waiting for transfers between devices, denoise(): lax.all_gather(jnp.concatenate([wq, wk, wv], axis=1), 'tile', axis=0, til...  58.9 us
    all_gather x1, blocking collectives, on_device(): modulation = lax.all_gather(local_mod, 'tile', axis=1, tiled=True)  23.3 us
    unnamed x48, local copies, waits for them, and re-layouts  19.5 us
    dot_general x1, matrix products, add_rows(): return jnp.dot(left, shard_rows, preferred_element_type=jnp.float32)  13.5 us
    slice x12, local copies, waits for them, and re-layouts, seam_blend(): term = taps(conv_w, shifted[b][:, a:a + rows], a, b)  11 us
    all_gather x1, waiting for transfers between devices, denoise(): lax.all_gather(wo, 'tile', axis=1, tiled=True)  10.2 us
    dot_general x18, matrix products, taps(): jnp.einsum('oc,c...->o...', conv_w[3 * a + b], window, precision=lax.Prec...  7.66 us
    dot_general x1, matrix products, denoise(): jnp.dot(mixed, lax.all_gather(wo, 'tile', axis=1, tiled=True), preferred_...  7.19 us
  transfers between devices with their start and end apart: 4, of which 2 were waited for; matrix products, arithmetic and copies ran while one was open for 27% of the time, Pallas kernels for 0%

profile of v3, /device:TPU:1, one launch (start us, length us, event | category | flops | bytes accessed | tf_op | source)
XLA Modules:
  0.0 239.8 jit_solution(10007489644422655267)
XLA Ops:
  7.2 2.1 pad_maximum_fusion
  12.8 1.5 copy.186
  15.9 1.5 convert_element_type.57
  18.0 3.7 %fusion.141 = (f32[3,256]{1,0:T(4,128)S(1)}, f32[3,256,2048]{2,1,0:T(8,128)}) fusion(f32[256,2048]{1,0:T(8,128)S(1)} %convert_element_type.57, bf16[128,2048]{1,0:T(8,128)(2,1)S(1)} %copy-done, bf16[3,256,128]{2,1,0:T(8,128)(2,1)S(1)} %gather_fusion, pred[3]{0:T(512)(128)(4,1)S(1)} %compare_and_fusion), kind=kOutput, calls=%fused_computation.218 | convolution fusion | flops 405896448 | bytes 9112579 | tf_op jit(solution)/shard_map/dot_general | solution.py:79
  21.7 3.8 %multiply_reduce_fusion.1 = f32[3,256]{1,0:T(4,128)S(1)} fusion(f32[3,256,2048]{2,1,0:T(8,128)} %get-tuple-element.77, f32[3,256]{1,0:T(4,128)S(1)} %broadcast_multiply_fusion.1), kind=kLoop, calls=%fused_computation.13 | loop fusion | flops 4717824 | bytes 6297600 | tf_op jit(solution)/shard_map/reduce_sum | solution.py:30
  25.7 23.3 %all-gather.1 = f32[16,1,384]{2,1,0:T(1,128)S(1)} all-gather(f32[1,1,384]{2,1,0:T(1,128)S(1)} %convolution_bitcast_fusion), channel_id=2, replica_groups=mesh['grp'=2,'tile'=16] {'tile'}, dimensions={0}, use_global_device_ids=true | all-gather | bytes 26112 | tf_op jit(solution)/shard_map/all_gather | solution.py:188
  49.2 5.6 %fusion.4 = bf16[768,2048]{1,0:T(8,128)(2,1)} fusion(f32[3,256,2048]{2,1,0:T(8,128)} %get-tuple-element.77, f32[2048]{0:T(1024)S(1)} %bitcast.163, f32[2048]{0:T(1024)S(1)} %bitcast.162, f32[768]{0:T(1024)S(1)} %rsqrt.36, f32[768]{0:T(1024)S(1)} %div.60), kind=kLoop, calls=%fused_computation.8 | loop fusion | flops 7864320 | bytes 9459712 | tf_op jit(solution)/shard_map/convert_element_type | solution.py:83
  54.8 58.9 %all-gather.5.cloned.1.call-done = bf16[2048,3072]{1,0:T(8,128)(2,1)} async-done(((bf16[128,3072]{1,0:T(8,128)(2,1)}), bf16[2048,3072]{1,0:T(8,128)(2,1)}) %all-gather.5.cloned.1.call-update) | async-done | bytes 12582928 | tf_op jit(solution)/shard_map/all_gather | solution.py:89
  113.7 13.5 %fusion.144 = f32[768,3072]{1,0:T(8,128)S(1)} fusion(bf16[768,2048]{1,0:T(8,128)(2,1)} %fusion.4, bf16[2048,3072]{1,0:T(8,128)(2,1)} %all-gather.5.cloned.1.call-done), kind=kOutput, calls=%fused_computation.221 | convolution fusion | flops 9663676416 | bytes 25165824 | tf_op jit(solution)/shard_map/dot_general | solution.py:58
  127.2 2.8 %slice_bitcast_fusion.1 = (f32[96,8,8,128]{3,1,2,0:T(8,128)S(1)}, f32[96,8,8,128]{3,1,2,0:T(8,128)}) fusion(f32[768,3072]{1,0:T(8,128)S(1)} %fusion.144), kind=kLoop, calls=%fused_computation.42 | loop fusion | bytes 12582912
  130.0 1.9 copy-done.6
  132.7 1.6 copy-done.2
  135.5 2.6 %copy.230 = f32[96,8,8,128]{3,2,1,0:T(8,128)S(1)} copy(f32[96,8,8,128]{3,1,2,0:T(8,128)} %get-tuple-element.18) | data formatting | bytes 6291456
  138.2 1.7 copy-done.4
  141.1 2.8 %fusion.20 = bf16[96,8,8,128]{3,1,2,0:T(8,128)(2,1)S(1)} fusion(f32[768,3072]{1,0:T(8,128)} %copy-done.6), kind=kLoop, calls=%fused_computation.52 | loop fusion | bytes 3145728
  148.3 4.8 %fusion.142 = (f32[3,8,256]{2,1,0:T(8,128)S(1)}, f32[3,8,256,256]{2,3,1,0:T(8,128)S(1)}) fusion(f32[3,8,256,256]{2,3,1,0:T(8,128)S(1)} %fusion.24), kind=kOutput, calls=%fused_computation.219 | output fusion | flops 6291711 | bytes 12607488 | tf_op jit(solution)/shard_map/sub | solution.py:101
  153.1 2.0 fusion.27
  155.1 2.0 copy.196
  157.1 10.2 %all-gather.7.cloned.1.call-done = bf16[1024,2048]{1,0:T(8,128)(2,1)} async-done(((bf16[1024,128]{1,0:T(8,128)(2,1)}), bf16[1024,2048]{1,0:T(8,128)(2,1)}) %all-gather.7.cloned.1.call-update) | async-done | bytes 4194320 | tf_op jit(solution)/shard_map/all_gather | solution.py:106
  167.3 7.2 %fusion.143 = (f32[768]{0:T(1024)S(1)}, f32[768,2048]{1,0:T(8,128)S(1)}) fusion(bf16[1024,2048]{1,0:T(8,128)(2,1)} %all-gather.7.cloned.1.call-done, bf16[96,8,8,128]{3,2,1,0:T(8,128)(2,1)S(1)} %bitcast.159, f32[2048]{0:T(1024)S(1)} %bitcast.164, f32[3,256,2048]{2,1,0:T(8,128)} %get-tuple-element.77), kind=kOutput, calls=%fused_computation.220 | convolution fusion | flops 3225943296 | bytes 18361344 | tf_op jit(solution)/shard_map/dot_general | solution.py:105
  179.9 1.4 copy.199
  181.3 1.8 copy_select_fusion
  183.1 3.5 %pad_slice_fusion.10 = (f32[32,34,2]{2,0,1:T(8,128)}, f32[32,34,2]{2,0,1:T(8,128)}, f32[32,34,2]{2,0,1:T(8,128)}, f32[32,34,2]{2,0,1:T(8,128)}, f32[32,34,2]{2,0...) fusion(f32[32,32,128]{2,0,1:T(8,128)S(1)} %copy_select_fusion), kind=kLoop, calls=%fused_computation.26 | loop fusion | bytes 602624 | tf_op jit(solution)/shard_map/slice | solution.py:130
  187.9 2.1 stack.48
  197.8 1.9 stack.49
  207.6 1.8 stack.50
  211.1 1.6 fusion.39
  212.8 1.7 fusion.134
  215.2 3.2 %collective-permute-start = (f32[32,1,128]{2,0,1:T(8,128)S(1)}, f32[32,1,128]{2,0,1:T(8,128)S(1)}, u32[]{:S(2)}, u32[]{:S(2)}) collective-permute-start(f32[32,1,128]{2,0,1:T(8,128)S(1)} %get-tuple-element.50), channel_id=1, source_target_pairs={{0,1},{1,2},{2,3},{3,4},{4,5},{5,6},{6,7},{7,8},{8,9},{9,10},{10,1... | collective-permute-start | bytes 49160 | tf_op jit(solution)/shard_map/ppermute | solution.py:125
  218.3 2.2 collective-permute-start.1
  221.9 4.6 %concatenate.21 = f32[32,32,128]{2,0,1:T(8,128)} concatenate(f32[32,32,1]{2,0,1:T(8,128)S(1)} %copy.219, f32[32,32,30]{2,0,1:T(8,128)} %get-tuple-element.33, f32[32,32,2]{2,0,1:T(8,128)S(1)} %copy.220, f32[32,32,30]{2,0,1:T(8,128)} %get-tuple-element.32, f32[32,32,2]{2,0,1:T(8,128)S(1)} %copy.221, f32[32,32,30]{2,0,1:T(8,128)} %get-tuple-element.31, f32[32,32,2]{2,0,1:T(8,128)S(1)} %copy.222, ...), dimensions={2} | concatenate | bytes 1048576 | tf_op jit(solution)/shard_map/concatenate | solution.py:155
  229.3 1.4 fusion.34
  (132 shorter events, 43.5 us)
Async XLA Ops:
  7.2 10.8 %copy-start = (bf16[128,2048]{1,0:T(8,128)(2,1)S(1)}, bf16[128,2048]{1,0:T(8,128)(2,1)}, u32[]{:S(2)}) copy-start(bf16[128,2048]{1,0:T(8,128)(2,1)} %param.22) | copy-start | bytes 1572868
  7.2 106.6 %all-gather.5.cloned.1.call-start = ((), (), s32[]{:S(2)}) async-start(), calls=%async_computation | async-start | bytes 13369344 | tf_op jit(solution)/shard_map/all_gather | solution.py:89
  9.3 158.0 %all-gather.7.cloned.1.call-start = ((), (), s32[]{:S(2)}) async-start(), calls=%async_computation.1 | async-start | bytes 4456448 | tf_op jit(solution)/shard_map/all_gather | solution.py:106
  21.7 3.8 %copy-start.16 = (bf16[256,384]{1,0:T(8,128)(2,1)S(1)}, bf16[256,384]{1,0:T(8,128)(2,1)}, u32[]{:S(2)}) copy-start(bf16[256,384]{1,0:T(8,128)(2,1)} %param.23) | copy-start | bytes 589828
  127.2 4.7 %copy-start.6 = (f32[768,3072]{1,0:T(8,128)}, f32[768,3072]{1,0:T(8,128)S(1)}, u32[]{:S(2)}) copy-start(f32[768,3072]{1,0:T(8,128)S(1)} %fusion.144) | copy-start | bytes 28311556
  132.7 1.7 copy-start.2
  138.2 1.7 copy-start.4
  141.1 3.3 %copy-start.3 = (f32[96,8,8,128]{3,2,1,0:T(8,128)S(1)}, f32[96,8,8,128]{3,2,1,0:T(8,128)}, u32[]{:S(2)}) copy-start(f32[96,8,8,128]{3,2,1,0:T(8,128)} %copy-done.2) | copy-start | bytes 9437188
  141.1 3.3 %copy-start.18 = (f32[128]{0:T(128)S(1)}, f32[128]{0:T(128)}, u32[]{:S(2)}) copy-start(f32[128]{0:T(128)} %param.28) | copy-start | bytes 1540
  144.3 1.9 copy-start.5
  144.3 1.9 copy-start.19
  174.5 1.0 copy-start.15
  178.7 2.5 %copy-start.9 = (f32[32,32,128]{2,1,0:T(8,128)S(1)}, f32[32,32,128]{2,1,0:T(8,128)}, u32[]{:S(2)}) copy-start(f32[32,32,128]{2,1,0:T(8,128)} %param.16) | copy-start | bytes 1572868
  187.9 5.9 %copy-start.10 = (f32[9,32,32]{2,1,0:T(8,128)S(1)}, f32[9,32,32]{2,1,0:T(8,128)}, u32[]{:S(2)}) copy-start(f32[9,32,32]{2,1,0:T(8,128)} %param.31) | copy-start | bytes 110596
  199.7 7.9 %copy-start.7 = (f32[32,34,2]{2,0,1:T(8,128)S(1)}, f32[32,34,2]{2,0,1:T(8,128)}, u32[]{:S(2)}) copy-start(f32[32,34,2]{2,0,1:T(8,128)} %get-tuple-element.43) | copy-start | bytes 26116
  199.7 7.8 %copy-start.8 = (f32[32,34,2]{2,0,1:T(8,128)S(1)}, f32[32,34,2]{2,0,1:T(8,128)}, u32[]{:S(2)}) copy-start(f32[32,34,2]{2,0,1:T(8,128)} %get-tuple-element.44) | copy-start | bytes 26116
  209.4 1.7 copy-start.11
  209.4 1.7 copy-start.12
  209.4 1.7 copy-start.13
  209.4 1.7 copy-start.14
  215.2 12.4 %collective-permute-start = (f32[32,1,128]{2,0,1:T(8,128)S(1)}, f32[32,1,128]{2,0,1:T(8,128)S(1)}, u32[]{:S(2)}, u32[]{:S(2)}) collective-permute-start(f32[32,1,128]{2,0,1:T(8,128)S(1)} %get-tuple-element.50), channel_id=1, source_target_pairs={{0,1},{1,2},{2,3},{3,4},{4,5},{5,6},{6,7},{7,8},{8,9},{9,10},{10,1... | collective-permute-start | bytes 49160 | tf_op jit(solution)/shard_map/ppermute | solution.py:125
  218.3 9.3 %collective-permute-start.1 = (f32[32,1,128]{2,0,1:T(8,128)S(1)}, f32[32,1,128]{2,0,1:T(8,128)S(1)}, u32[]{:S(2)}, u32[]{:S(2)}) collective-permute-start(f32[32,1,128]{2,0,1:T(8,128)S(1)} %get-tuple-element.49), channel_id=1, source_target_pairs={{1,0},{2,1},{3,2},{4,3},{5,4},{6,5},{7,6},{8,7},{9,8},{10,9},{11,1... | collective-permute-start | bytes 49160 | tf_op jit(solution)/shard_map/ppermute | solution.py:126
  221.9 6.1 %copy-start.17 = (f32[32,1,128]{2,0,1:T(8,128)S(1)}, f32[32,1,128]{2,0,1:T(8,128)}, u32[]{:S(2)}) copy-start(f32[32,1,128]{2,0,1:T(8,128)} %get-tuple-element.48) | copy-start | bytes 49156
  226.4 6.5 %copy-start.1 = (bf16[128,2048]{1,0:T(8,128)(2,1)S(1)}, bf16[128,2048]{1,0:T(8,128)(2,1)}, u32[]{:S(2)}) copy-start(bf16[128,2048]{1,0:T(8,128)(2,1)} %param.22) | copy-start | bytes 1572868
Sparse Core Ops, SparseCore 0:
  10.3 103.3 all-gather.4
  115.9 51.3 all-gather.6

commit v4 on v1

--- a/solution.py
+++ b/solution.py
@@ -65,6 +65,12 @@
     return jnp.transpose(shaped, (5, 1, 3, 0, 2, 4)).reshape(
         channels, tile_side * PATCH, tiles_here * tile_side * PATCH
     )
+
+
+def share_of_part(w_local):
+    parts = lax.axis_size("grp")
+    rows = w_local.shape[0] // parts
+    return lax.dynamic_slice_in_dim(w_local, lax.axis_index("grp") * rows, rows, axis=0)
 
 
 def add_rows(left, shard_rows):
@@ -99,7 +105,7 @@
         return add_rows(modulated, shard_rows)
 
     inner = wq.shape[1]
-    qkv = lax.all_gather(jnp.concatenate([wq, wk, wv], axis=1), "tile", axis=0, tiled=True)
+    qkv = lax.all_gather(share_of_part(jnp.concatenate([wq, wk, wv], axis=1)), ("tile", "grp"), axis=0, tiled=True)
     qkv_all = add_one(qkv)
     query_all = qkv_all[:, :inner]
     key_all = qkv_all[:, inner : 2 * inner]

time: 206 us -> 203 us (0.985)
  waiting for transfers between devices: 72.9 us -> 70 us
    all_gather x1, waiting for transfers between devices: 59 us -> 56 us  [denoise(): lax.all_gather(share_of_part(jnp.concatenate([wq, wk, wv], axis=1)), ('ti...]
where the time goes in v4:
time: 203 us; the launch traced here: 202 us
  waiting for transfers between devices  70 us (34%)
  matrix products  34.3 us (17%)
  local copies, waits for them, and re-layouts  27.2 us (13%)
  other arithmetic  27 us (13%)
  blocking collectives  23 us (11%)
  between operations  15.5 us (8%)
  starting transfers between devices  5.16 us (3%)
    all_gather x1, waiting for transfers between devices, denoise(): lax.all_gather(share_of_part(jnp.concatenate([wq, wk, wv], axis=1)), ('ti...  56 us
    all_gather x1, blocking collectives, on_device(): modulation = lax.all_gather(local_mod, 'tile', axis=1, tiled=True)  23 us
    unnamed x36, local copies, waits for them, and re-layouts  19.4 us
    dot_general x1, matrix products, add_rows(): return jnp.dot(left, shard_rows, preferred_element_type=jnp.float32)  13.5 us
    all_gather x1, waiting for transfers between devices, denoise(): lax.all_gather(wo, 'tile', axis=1, tiled=True)  10.4 us
    dot_general x1, matrix products, denoise(): jnp.dot(mixed, lax.all_gather(wo, 'tile', axis=1, tiled=True), preferred_...  7.19 us
    dot_general x9, matrix products, on_device(): jnp.einsum('oc,chw->ohw', conv_w[3 * row_shift + col_shift], window, prec...  5.81 us
    convert_element_type x1, other arithmetic, denoise(): (layer_norm(hidden0) * (1.0 + scale_vec) + shift_vec).astype(jnp.bfloat16)  5.58 us
  transfers between devices with their start and end apart: 4, of which 3 were waited for; matrix products, arithmetic and copies ran while one was open for 28% of the time, Pallas kernels for 0%

profile of v4, /device:TPU:1, one launch (start us, length us, event | category | flops | bytes accessed | tf_op | source)
XLA Modules:
  0.0 202.2 jit_solution(11390709639415344935)
XLA Ops:
  7.2 1.9 fusion.53
  12.4 1.5 copy.83
  13.9 1.1 copy.84
  15.6 1.5 convert_element_type.55
  17.7 3.6 %fusion.85 = (f32[3,256]{1,0:T(4,128)S(1)}, f32[3,256,2048]{2,1,0:T(8,128)}) fusion(f32[256,2048]{1,0:T(8,128)S(1)} %convert_element_type.55, bf16[128,2048]{1,0:T(8,128)(2,1)S(1)} %copy-done, bf16[3,256,128]{2,1,0:T(8,128)(2,1)S(1)} %gather_fusion, pred[3]{0:T(512)(128)(4,1)S(1)} %compare_and_fusion), kind=kOutput, calls=%fused_computation.146 | convolution fusion | flops 405896448 | bytes 9112579 | tf_op jit(solution)/shard_map/dot_general | solution.py:98
  21.3 3.9 %multiply_reduce_fusion.1 = f32[3,256]{1,0:T(4,128)S(1)} fusion(f32[3,256,2048]{2,1,0:T(8,128)} %get-tuple-element.26, f32[3,256]{1,0:T(4,128)S(1)} %broadcast_multiply_fusion.1), kind=kLoop, calls=%fused_computation.13 | loop fusion | flops 4717824 | bytes 6297600 | tf_op jit(solution)/shard_map/reduce_sum | solution.py:43
  25.4 23.0 %all-gather.1 = f32[16,1,384]{2,1,0:T(1,128)S(1)} all-gather(f32[1,1,384]{2,1,0:T(1,128)S(1)} %convolution_bitcast_fusion), channel_id=2, replica_groups=mesh['grp'=2,'tile'=16] {'tile'}, dimensions={0}, use_global_device_ids=true | all-gather | bytes 26112 | tf_op jit(solution)/shard_map/all_gather | solution.py:160
  48.6 5.6 %fusion.4 = bf16[768,2048]{1,0:T(8,128)(2,1)} fusion(f32[3,256,2048]{2,1,0:T(8,128)} %get-tuple-element.26, f32[2048]{0:T(1024)S(1)} %bitcast.139, f32[2048]{0:T(1024)S(1)} %bitcast.138, f32[768]{0:T(1024)S(1)} %rsqrt.36, f32[768]{0:T(1024)S(1)} %div.60), kind=kLoop, calls=%fused_computation.8 | loop fusion | flops 7864320 | bytes 9459712 | tf_op jit(solution)/shard_map/convert_element_type | solution.py:102
  54.1 56.0 %all-gather.5.cloned.1.call-done = bf16[2048,3072]{1,0:T(8,128)(2,1)} async-done(((bf16[64,3072]{1,0:T(8,128)(2,1)}), bf16[2048,3072]{1,0:T(8,128)(2,1)}) %all-gather.5.cloned.1.call-update) | async-done | bytes 12582928 | tf_op jit(solution)/shard_map/all_gather | solution.py:108
  110.2 13.5 %fusion.88 = f32[768,3072]{1,0:T(8,128)S(1)} fusion(bf16[768,2048]{1,0:T(8,128)(2,1)} %fusion.4, bf16[2048,3072]{1,0:T(8,128)(2,1)} %all-gather.5.cloned.1.call-done), kind=kOutput, calls=%fused_computation.149 | convolution fusion | flops 9663676416 | bytes 25165824 | tf_op jit(solution)/shard_map/dot_general | solution.py:77
  123.7 2.8 %slice_bitcast_fusion.1 = (f32[96,8,8,128]{3,1,2,0:T(8,128)S(1)}, f32[96,8,8,128]{3,1,2,0:T(8,128)}) fusion(f32[768,3072]{1,0:T(8,128)S(1)} %fusion.88), kind=kLoop, calls=%fused_computation.29 | loop fusion | bytes 12582912
  126.4 1.9 copy-done.6
  129.1 1.6 copy-done.2
  131.9 2.6 %copy.104 = f32[96,8,8,128]{3,2,1,0:T(8,128)S(1)} copy(f32[96,8,8,128]{3,1,2,0:T(8,128)} %get-tuple-element.18) | data formatting | bytes 6291456
  134.6 1.7 copy-done.4
  137.5 2.8 %fusion.20 = bf16[96,8,8,128]{3,1,2,0:T(8,128)(2,1)S(1)} fusion(f32[768,3072]{1,0:T(8,128)} %copy-done.6), kind=kLoop, calls=%fused_computation.41 | loop fusion | bytes 3145728
  140.8 1.0 fusion.14
  142.6 1.0 fusion.11
  144.6 4.8 %fusion.86 = (f32[3,8,256]{2,1,0:T(8,128)S(1)}, f32[3,8,256,256]{2,3,1,0:T(8,128)S(1)}) fusion(f32[3,8,256,256]{2,3,1,0:T(8,128)S(1)} %fusion.24), kind=kOutput, calls=%fused_computation.147 | output fusion | flops 6291711 | bytes 12607488 | tf_op jit(solution)/shard_map/sub | solution.py:120
  149.4 2.0 fusion.27
  151.4 2.0 copy.93
  153.4 10.4 %all-gather.7.cloned.1.call-done = bf16[1024,2048]{1,0:T(8,128)(2,1)} async-done(((bf16[1024,128]{1,0:T(8,128)(2,1)}), bf16[1024,2048]{1,0:T(8,128)(2,1)}) %all-gather.7.cloned.1.call-update) | async-done | bytes 4194320 | tf_op jit(solution)/shard_map/all_gather | solution.py:125
  163.8 7.2 %fusion.87 = (f32[768]{0:T(1024)S(1)}, f32[768,2048]{1,0:T(8,128)S(1)}) fusion(bf16[1024,2048]{1,0:T(8,128)(2,1)} %all-gather.7.cloned.1.call-done, bf16[96,8,8,128]{3,2,1,0:T(8,128)(2,1)S(1)} %bitcast.135, f32[2048]{0:T(1024)S(1)} %bitcast.140, f32[3,256,2048]{2,1,0:T(8,128)} %get-tuple-element.26), kind=kOutput, calls=%fused_computation.148 | convolution fusion | flops 3225943296 | bytes 18361344 | tf_op jit(solution)/shard_map/dot_general | solution.py:124
  172.1 1.1 fusion.33
  174.2 1.1 multiply_bitcast_fusion
  175.3 1.1 copy.94
  177.0 1.6 copy_select_fusion
  178.7 3.2 %collective-permute-start = (f32[32,1,128]{2,0,1:T(8,128)S(1)}, f32[32,1,128]{2,0,1:T(8,128)S(1)}, u32[]{:S(2)}, u32[]{:S(2)}) collective-permute-start(f32[32,1,128]{2,0,1:T(8,128)S(1)} %get-tuple-element.19), channel_id=1, source_target_pairs={{0,1},{1,2},{2,3},{3,4},{4,5},{5,6},{6,7},{7,8},{8,9},{9,10},{10,1... | collective-permute-start | bytes 49160 | tf_op jit(solution)/shard_map/ppermute | solution.py:20
  181.9 1.9 collective-permute-start.1
  184.0 2.9 %collective-permute-done.1 = f32[32,1,128]{2,0,1:T(8,128)S(1)} collective-permute-done((f32[32,1,128]{2,0,1:T(8,128)S(1)}, f32[32,1,128]{2,0,1:T(8,128)S(1)}, u32[]{:S(2)}, u32[]{:S(2)}) %collective-permute-start.1) | collective-permute-done | bytes 16416 | tf_op jit(solution)/shard_map/ppermute | solution.py:23
  193.2 1.1 copy.100
  194.3 1.1 copy.99
  (81 shorter events, 18.3 us)
Async XLA Ops:
  7.2 10.5 %copy-start = (bf16[128,2048]{1,0:T(8,128)(2,1)S(1)}, bf16[128,2048]{1,0:T(8,128)(2,1)}, u32[]{:S(2)}) copy-start(bf16[128,2048]{1,0:T(8,128)(2,1)} %param.22) | copy-start | bytes 1572868
  7.2 103.0 %all-gather.5.cloned.1.call-start = ((), (), s32[]{:S(2)}) async-start(), calls=%async_computation | async-start | bytes 12976128 | tf_op jit(solution)/shard_map/all_gather | solution.py:108
  9.1 154.7 %all-gather.7.cloned.1.call-start = ((), (), s32[]{:S(2)}) async-start(), calls=%async_computation.1 | async-start | bytes 4456448 | tf_op jit(solution)/shard_map/all_gather | solution.py:125
  21.3 3.9 %copy-start.10 = (bf16[256,384]{1,0:T(8,128)(2,1)S(1)}, bf16[256,384]{1,0:T(8,128)(2,1)}, u32[]{:S(2)}) copy-start(bf16[256,384]{1,0:T(8,128)(2,1)} %param.23) | copy-start | bytes 589828
  123.7 4.7 %copy-start.6 = (f32[768,3072]{1,0:T(8,128)}, f32[768,3072]{1,0:T(8,128)S(1)}, u32[]{:S(2)}) copy-start(f32[768,3072]{1,0:T(8,128)S(1)} %fusion.88) | copy-start | bytes 28311556
  129.1 1.6 copy-start.2
  134.6 1.7 copy-start.4
  137.5 3.3 %copy-start.3 = (f32[96,8,8,128]{3,2,1,0:T(8,128)S(1)}, f32[96,8,8,128]{3,2,1,0:T(8,128)}, u32[]{:S(2)}) copy-start(f32[96,8,8,128]{3,2,1,0:T(8,128)} %copy-done.2) | copy-start | bytes 9437188
  137.5 3.3 %copy-start.12 = (f32[128]{0:T(128)S(1)}, f32[128]{0:T(128)}, u32[]{:S(2)}) copy-start(f32[128]{0:T(128)} %param.28) | copy-start | bytes 1540
  140.7 1.9 copy-start.5
  140.7 1.9 copy-start.13
  171.0 1.0 copy-start.9
  175.3 1.8 copy-start.7
  176.4 10.8 %copy-start.11 = (f32[9,32,32]{2,1,0:T(8,128)S(1)}, f32[9,32,32]{2,1,0:T(8,128)}, u32[]{:S(2)}) copy-start(f32[9,32,32]{2,1,0:T(8,128)} %param.31) | copy-start | bytes 110596
  178.7 5.3 %collective-permute-start = (f32[32,1,128]{2,0,1:T(8,128)S(1)}, f32[32,1,128]{2,0,1:T(8,128)S(1)}, u32[]{:S(2)}, u32[]{:S(2)}) collective-permute-start(f32[32,1,128]{2,0,1:T(8,128)S(1)} %get-tuple-element.19), channel_id=1, source_target_pairs={{0,1},{1,2},{2,3},{3,4},{4,5},{5,6},{6,7},{7,8},{8,9},{9,10},{10,1... | collective-permute-start | bytes 49160 | tf_op jit(solution)/shard_map/ppermute | solution.py:20
  181.9 5.1 %collective-permute-start.1 = (f32[32,1,128]{2,0,1:T(8,128)S(1)}, f32[32,1,128]{2,0,1:T(8,128)S(1)}, u32[]{:S(2)}, u32[]{:S(2)}) collective-permute-start(f32[32,1,128]{2,0,1:T(8,128)S(1)} %get-tuple-element.20), channel_id=1, source_target_pairs={{1,0},{2,1},{3,2},{4,3},{5,4},{6,5},{7,6},{8,7},{9,8},{10,9},{11,1... | collective-permute-start | bytes 49160 | tf_op jit(solution)/shard_map/ppermute | solution.py:23
  189.8 2.5 %copy-start.8 = (f32[32,32,128]{2,1,0:T(8,128)S(1)}, f32[32,32,128]{2,1,0:T(8,128)}, u32[]{:S(2)}) copy-start(f32[32,32,128]{2,1,0:T(8,128)} %param.18) | copy-start | bytes 1572868
  191.7 3.7 %copy-start.1 = (bf16[128,2048]{1,0:T(8,128)(2,1)S(1)}, bf16[128,2048]{1,0:T(8,128)(2,1)}, u32[]{:S(2)}) copy-start(bf16[128,2048]{1,0:T(8,128)(2,1)} %param.22) | copy-start | bytes 1572868
Sparse Core Ops, SparseCore 0:
  11.5 98.6 all-gather.4
  112.3 51.4 all-gather.6

commit v5 on v4

--- a/solution.py
+++ b/solution.py
@@ -3,6 +3,8 @@
 import jax
 import jax.numpy as jnp
 from jax import lax
+from jax.experimental import pallas as pl
+from jax.experimental.pallas import tpu as pltpu
 from jax.sharding import PartitionSpec as P
 
 HD = 128
@@ -10,19 +12,6 @@
 MAXOWN = 3
 TSTEPS = 1000
 STRIDE = 20
-
-
-def padded_2(block, sides, width):
-    for axis, dim in sides:
-        count = lax.axis_size(axis)
-        forward = [(i, i + 1) for i in range(count - 1)]
-        backward = [(target, source) for source, target in forward]
-        low = lax.ppermute(
-            lax.slice_in_dim(block, block.shape[dim] - width, None, axis=dim), axis, forward
-        )
-        high = lax.ppermute(lax.slice_in_dim(block, 0, width, axis=dim), axis, backward)
-        block = jnp.concatenate([low, block, high], axis=dim)
-    return block
 
 
 def plan(step):
@@ -128,6 +117,52 @@
     final = layer_norm(hidden1).astype(jnp.bfloat16)
     eps_pred = jnp.dot(final, out_w, preferred_element_type=jnp.float32).astype(jnp.bfloat16)
     return eps_pred.reshape(count, tokens_tile, token_values)
+
+
+def finish_kernel(scale_ref, left_ref, mid_ref, right_ref, w_ref, noise_ref, est_ref, next_ref):
+    channels, pixels = est_ref.shape
+    cols = (left_ref.shape[1] - pixels) // 2
+    shifted = (left_ref, mid_ref, right_ref)
+    blended = None
+    for a in range(3):
+        for b in range(3):
+            window = shifted[b][:, a * cols : a * cols + pixels]
+            term = jnp.dot(
+                w_ref[3 * a + b], window,
+                precision=lax.Precision.HIGHEST, preferred_element_type=jnp.float32,
+            )
+            blended = term if blended is None else blended + term
+    raw = mid_ref[:, cols : cols + pixels]
+    place = lax.broadcasted_iota(jnp.int32, (1, pixels), 1)
+    row, col = place // cols, place % cols
+    tile_px = pixels // cols
+    seam = (row == 0) | (row == tile_px - 1) | (col % tile_px == 0) | (col % tile_px == tile_px - 1)
+    estimate = jnp.where(seam, blended, raw)
+    est_ref[...] = estimate
+    next_ref[...] = scale_ref[0] * estimate + scale_ref[1] * noise_ref[...]
+
+
+def seam_finish(raw, noise, conv_w, cos_prev, sin_prev):
+    channels, rows, cols = raw.shape
+    count = lax.axis_size("tile")
+    forward = [(i, i + 1) for i in range(count - 1)]
+    backward = [(target, source) for source, target in forward]
+    low = lax.ppermute(raw[:, rows - 1 :], "tile", forward)
+    high = lax.ppermute(raw[:, :1], "tile", backward)
+    framed = jnp.pad(jnp.concatenate([low, raw, high], axis=1), ((0, 0), (0, 0), (1, 1)))
+    shifted = [
+        framed[:, :, b : b + cols].reshape(channels, (rows + 2) * cols) for b in range(3)
+    ]
+    scale = jnp.stack([cos_prev, sin_prev]).astype(jnp.float32)
+    vmem = pl.BlockSpec(memory_space=pltpu.VMEM)
+    flat = jax.ShapeDtypeStruct((channels, rows * cols), jnp.float32)
+    estimate, next_latent = pl.pallas_call(
+        finish_kernel,
+        out_shape=(flat, flat),
+        in_specs=[pl.BlockSpec(memory_space=pltpu.SMEM)] + [vmem] * 5,
+        out_specs=(vmem, vmem),
+    )(scale, *shifted, conv_w, noise.reshape(channels, rows * cols))
+    return estimate.reshape(raw.shape), next_latent.reshape(raw.shape)
 
 
 def on_device(
@@ -191,25 +226,7 @@
     raw_estimate = jnp.where(
         cloud_cols[None, None, :], (latent - sin_now * eps_latent) / cos_now, observed
     )
-    padded = padded_2(raw_estimate, (("tile", 1),), 1)
-    padded = jnp.pad(padded, ((0, 0), (0, 0), (1, 1)))
-    blended = jnp.zeros_like(raw_estimate)
-    for row_shift in range(3):
-        for col_shift in range(3):
-            window = padded[:, row_shift : row_shift + band_rows, col_shift : col_shift + band_cols]
-            blended = blended + jnp.einsum(
-                "oc,chw->ohw",
-                conv_w[3 * row_shift + col_shift],
-                window,
-                precision=lax.Precision.HIGHEST,
-            )
-    row_pos = jnp.arange(band_rows) % band_rows
-    col_pos = jnp.arange(band_cols) % band_rows
-    seam_mask = ((row_pos == 0) | (row_pos == band_rows - 1))[:, None] | (
-        (col_pos == 0) | (col_pos == band_rows - 1)
-    )[None, :]
-    estimate = jnp.where(seam_mask[None], blended, raw_estimate)
-    next_latent = cos_prev * estimate + sin_prev * noise
+    estimate, next_latent = seam_finish(raw_estimate, noise, conv_w, cos_prev, sin_prev)
     return (estimate, next_latent)
 
 

time: 203 us -> 217 us (1.069)
  local copies, waits for them, and re-layouts: 27.2 us -> 46.9 us
  waiting for transfers between devices: 70 us -> 58.7 us
  Pallas kernels: 0 us -> 6.38 us
  matrix products: 34.3 us -> 31.1 us
  other arithmetic: 27 us -> 29.2 us
    all_gather x1, waiting for transfers between devices: 56 us -> 46.8 us  [denoise(): lax.all_gather(share_of_part(jnp.concatenate([wq, wk, wv], axis=1)), ('ti...]
    reshape x0 -> x3, local copies, waits for them, and re-layouts: none -> 7.53 us  [seam_finish(): framed[:, :, b:b + cols].reshape(channels, (rows + 2) * cols)]
    pallas_call x0 -> x1, Pallas kernels: none -> 6.38 us  [seam_finish(): pl.pallas_call(finish_kernel, out_shape=(flat, flat), in_specs=[pl.BlockS...]
    dot_general x9 -> x0, matrix products: 5.81 us -> none  [on_device(): jnp.einsum('oc,chw->ohw', conv_w[3 * row_shift + col_shift], window, prec...]
    unnamed x36 -> x38, local copies, waits for them, and re-layouts: 19.4 us -> 24.3 us
    slice x1 -> x2, local copies, waits for them, and re-layouts: 0.01 us -> 2.7 us  [the longest x1 2.69 us: seam_finish(): framed[:, :, b:b + cols].reshape(channels, (rows + 2) * cols)]
    reshape x1, local copies, waits for them, and re-layouts: 0.51 us -> 2.89 us  [band_tiles(): jnp.transpose(shaped, (3, 1, 4, 2, 5, 0))]
  transfers between devices with their start and end apart: 4 -> 4, of which waited for: 3 -> 3; matrix products, arithmetic and copies ran while one was open for 28% -> 32% of each run, Pallas kernels for 0% -> 0%
where the time goes in v5:
time: 217 us
  waiting for transfers between devices  58.7 us (27%)
  local copies, waits for them, and re-layouts  46.9 us (22%)
  matrix products  31.1 us (14%)
  other arithmetic  29.2 us (13%)
  blocking collectives  23.5 us (11%)
  between operations  15.4 us (7%)
  Pallas kernels  6.38 us (3%)
  starting transfers between devices  5.42 us (2%)
    all_gather x1, waiting for transfers between devices, denoise(): lax.all_gather(share_of_part(jnp.concatenate([wq, wk, wv], axis=1)), ('ti...  46.8 us
    unnamed x38, local copies, waits for them, and re-layouts  24.3 us
    all_gather x1, blocking collectives, on_device(): modulation = lax.all_gather(local_mod, 'tile', axis=1, tiled=True)  23.5 us
    dot_general x1, matrix products, add_rows(): return jnp.dot(left, shard_rows, preferred_element_type=jnp.float32)  13.5 us
    all_gather x1, waiting for transfers between devices, denoise(): lax.all_gather(wo, 'tile', axis=1, tiled=True)  9.49 us
    dot_general x1, matrix products, denoise(): jnp.dot(mixed, lax.all_gather(wo, 'tile', axis=1, tiled=True), preferred_...  8.03 us
    reshape x3, local copies, waits for them, and re-layouts, seam_finish(): framed[:, :, b:b + cols].reshape(channels, (rows + 2) * cols)  7.53 us
    pallas_call x1, Pallas kernels, seam_finish(): pl.pallas_call(finish_kernel, out_shape=(flat, flat), in_specs=[pl.BlockS...  6.38 us
  transfers between devices with their start and end apart: 4, of which 3 were waited for; matrix products, arithmetic and copies ran while one was open for 32% of the time, Pallas kernels for 0%

profile of v5, /device:TPU:1, one launch (start us, length us, event | category | flops | bytes accessed | tf_op | source)
XLA Modules:
  0.0 216.6 jit_solution(5164683434784430957)
XLA Ops:
  7.2 1.9 fusion.33
  12.5 1.7 copy.89
  14.4 2.2 %copy.78 = bf16[4,16,16,2,2,32]{5,4,3,2,1,0:T(2,128)(2,1)} copy(bf16[4,16,16,2,2,32]{5,4,2,0,3,1:T(2,128)(2,1)S(1)} %bitcast.106) | data formatting | bytes 524288 | tf_op jit(solution)/shard_map/transpose | solution.py:46
  16.6 2.9 %reshape.205 = bf16[4,256,128]{2,1,0:T(8,128)(2,1)S(1)} reshape(bf16[4,16,16,2,2,32]{5,4,3,2,1,0:T(2,128)(2,1)} %copy.78) | data formatting | bytes 524288 | tf_op jit(solution)/shard_map/reshape | solution.py:46
  19.5 2.8 %convert_element_type.55 = f32[256,2048]{1,0:T(8,128)} convert(bf16[256,2048]{1,0:T(8,128)(2,1)} %param.21) | non-fusion elementwise | flops 524288 | bytes 3145728 | tf_op jit(solution)/shard_map/convert_element_type | solution.py:90
  22.9 5.3 %fusion.45 = (f32[3,256]{1,0:T(4,128)S(1)}, f32[3,256,2048]{2,1,0:T(8,128)}) fusion(f32[256,2048]{1,0:T(8,128)} %convert_element_type.55, bf16[128,2048]{1,0:T(8,128)(2,1)S(1)} %copy-done, bf16[3,256,128]{2,1,0:T(8,128)(2,1)S(1)} %gather_fusion, pred[3]{0:T(512)(128)(4,1)S(1)} %compare_and_fusion), kind=kOutput, calls=%fused_computation.93 | convolution fusion | flops 405896448 | bytes 9112579 | tf_op jit(solution)/shard_map/dot_general | solution.py:87
  28.2 3.6 %multiply_reduce_fusion.1 = f32[3,256]{1,0:T(4,128)S(1)} fusion(f32[3,256,2048]{2,1,0:T(8,128)} %get-tuple-element.20, f32[3,256]{1,0:T(4,128)S(1)} %broadcast_multiply_fusion.1), kind=kLoop, calls=%fused_computation.13 | loop fusion | flops 4717824 | bytes 6297600 | tf_op jit(solution)/shard_map/reduce_sum | solution.py:32
  32.1 23.5 %all-gather.1 = f32[16,1,384]{2,1,0:T(1,128)S(1)} all-gather(f32[1,1,384]{2,1,0:T(1,128)S(1)} %convolution_bitcast_fusion), channel_id=2, replica_groups=mesh['grp'=2,'tile'=16] {'tile'}, dimensions={0}, use_global_device_ids=true | all-gather | bytes 26112 | tf_op jit(solution)/shard_map/all_gather | solution.py:195
  55.7 2.0 copy.90
  57.7 5.6 %fusion.4 = bf16[768,2048]{1,0:T(8,128)(2,1)} fusion(f32[3,256,2048]{2,1,0:T(8,128)} %get-tuple-element.20, f32[2048]{0:T(1024)S(1)} %bitcast.118, f32[2048]{0:T(1024)S(1)} %bitcast.117, f32[768]{0:T(1024)S(1)} %rsqrt.36, f32[768]{0:T(1024)S(1)} %div.61), kind=kLoop, calls=%fused_computation.8 | loop fusion | flops 7864320 | bytes 9459712 | tf_op jit(solution)/shard_map/convert_element_type | solution.py:91
  63.3 46.8 %all-gather.5.cloned.1.call-done = bf16[2048,3072]{1,0:T(8,128)(2,1)} async-done(((bf16[64,3072]{1,0:T(8,128)(2,1)}), bf16[2048,3072]{1,0:T(8,128)(2,1)}) %all-gather.5.cloned.1.call-update) | async-done | bytes 12582928 | tf_op jit(solution)/shard_map/all_gather | solution.py:97
  110.0 13.5 %fusion.48 = f32[768,3072]{1,0:T(8,128)S(1)} fusion(bf16[768,2048]{1,0:T(8,128)(2,1)} %fusion.4, bf16[2048,3072]{1,0:T(8,128)(2,1)} %all-gather.5.cloned.1.call-done), kind=kOutput, calls=%fused_computation.96 | convolution fusion | flops 9663676416 | bytes 25165824 | tf_op jit(solution)/shard_map/dot_general | solution.py:66
  123.5 2.8 %slice_bitcast_fusion.1 = (f32[96,8,8,128]{3,1,2,0:T(8,128)S(1)}, f32[96,8,8,128]{3,1,2,0:T(8,128)}) fusion(f32[768,3072]{1,0:T(8,128)S(1)} %fusion.48), kind=kLoop, calls=%fused_computation.29 | loop fusion | bytes 12582912
  126.3 1.9 copy-done.7
  131.8 2.6 %copy.100 = f32[96,8,8,128]{3,2,1,0:T(8,128)S(1)} copy(f32[96,8,8,128]{3,1,2,0:T(8,128)} %get-tuple-element.10) | data formatting | bytes 6291456
  134.4 1.7 copy-done.4
  137.3 2.8 %fusion.20 = bf16[96,8,8,128]{3,1,2,0:T(8,128)(2,1)S(1)} fusion(f32[768,3072]{1,0:T(8,128)} %copy-done.7), kind=kLoop, calls=%fused_computation.43 | loop fusion | bytes 3145728
  144.5 4.8 %fusion.46 = (f32[3,8,256]{2,1,0:T(8,128)S(1)}, f32[3,8,256,256]{2,3,1,0:T(8,128)S(1)}) fusion(f32[3,8,256,256]{2,3,1,0:T(8,128)S(1)} %fusion.24), kind=kOutput, calls=%fused_computation.94 | output fusion | flops 6291711 | bytes 12607488 | tf_op jit(solution)/shard_map/sub | solution.py:109
  149.3 2.1 fusion.27
  151.4 2.8 %copy.87 = bf16[3,256,8,128]{3,2,1,0:T(8,128)(2,1)} copy(bf16[3,256,8,128]{1,3,2,0:T(8,128)(2,1)} %fusion.27) | data formatting | bytes 3145728 | tf_op jit(solution)/shard_map/convert_element_type | solution.py:112
  154.2 9.5 %all-gather.7.cloned.1.call-done = bf16[1024,2048]{1,0:T(8,128)(2,1)} async-done(((bf16[1024,128]{1,0:T(8,128)(2,1)}), bf16[1024,2048]{1,0:T(8,128)(2,1)}) %all-gather.7.cloned.1.call-update) | async-done | bytes 4194320 | tf_op jit(solution)/shard_map/all_gather | solution.py:114
  163.7 8.0 %fusion.47 = (f32[768]{0:T(1024)S(1)}, f32[768,2048]{1,0:T(8,128)S(1)}) fusion(bf16[1024,2048]{1,0:T(8,128)(2,1)} %all-gather.7.cloned.1.call-done, bf16[96,8,8,128]{3,2,1,0:T(8,128)(2,1)} %bitcast.109, f32[2048]{0:T(1024)S(1)} %bitcast.119, f32[3,256,2048]{2,1,0:T(8,128)} %get-tuple-element.20), kind=kOutput, calls=%fused_computation.95 | convolution fusion | flops 3225943296 | bytes 18361344 | tf_op jit(solution)/shard_map/dot_general | solution.py:113
  175.8 2.4 %multiply_bitcast_fusion = f32[32,16,2,4,16,2]{0,5,2,4,1,3:T(2,128)S(1)} fusion(pred[4]{0:T(512)(128)(4,1)S(1)} %get-tuple-element.18, f32[]{:T(128)S(6)} %sin.10, bf16[4,16,16,2,2,32]{5,4,3,2,1,0:T(2,128)(2,1)} %gather.12, pred[4]{0:T(512)(128)(4,1)S(1)} %get-tuple-element.6), kind=kLoop, calls=%fused_computation.39 | loop fusion | flops 524288 | bytes 786444 | tf_op jit(solution)/shard_map/mul | solution.py:227
  180.2 3.2 %collective-permute-start = (f32[32,1,128]{0,2,1:T(8,128)S(1)}, f32[32,1,128]{0,2,1:T(8,128)S(1)}, u32[]{:S(2)}, u32[]{:S(2)}) collective-permute-start(f32[32,1,128]{0,2,1:T(8,128)S(1)} %get-tuple-element.13), channel_id=1, source_target_pairs={{0,1},{1,2},{2,3},{3,4},{4,5},{5,6},{6,7},{7,8},{8,9},{9,10},{10,1... | collective-permute-start | bytes 49160 | tf_op jit(solution)/shard_map/ppermute | solution.py:150
  183.4 2.2 %collective-permute-start.1 = (f32[32,1,128]{0,2,1:T(8,128)S(1)}, f32[32,1,128]{0,2,1:T(8,128)S(1)}, u32[]{:S(2)}, u32[]{:S(2)}) collective-permute-start(f32[32,1,128]{0,2,1:T(8,128)S(1)} %get-tuple-element.14), channel_id=1, source_target_pairs={{1,0},{2,1},{3,2},{4,3},{5,4},{6,5},{7,6},{8,7},{9,8},{10,9},{11,1... | collective-permute-start | bytes 49160 | tf_op jit(solution)/shard_map/ppermute | solution.py:151
  187.3 1.7 collective-permute-done.1
  189.3 2.7 %pad_slice_fusion = (f32[32,34,128]{0,2,1:T(8,128)}, f32[32,34,128]{0,2,1:T(8,128)}) fusion(f32[32,34,128]{0,2,1:T(8,128)S(1)} %pad_maximum_fusion), kind=kLoop, calls=%fused_computation.35 | loop fusion | bytes 1671168 | tf_op jit(solution)/shard_map/slice | solution.py:154
  192.0 3.0 %copy.95.left_ref = f32[32,4352]{1,0:T(8,128)} copy(f32[32,4352]{0,1:T(8,128)} %bitcast.104) | data formatting | bytes 1114112 | tf_op jit(solution)/shard_map/reshape | solution.py:154
  195.0 3.1 %copy.97.right_ref = f32[32,4352]{1,0:T(8,128)} copy(f32[32,4352]{0,1:T(8,128)} %bitcast.103) | data formatting | bytes 1114112 | tf_op jit(solution)/shard_map/reshape | solution.py:154
  199.5 6.4 %shard_map.167 = (f32[32,4096]{1,0:T(8,128)}, f32[32,4096]{1,0:T(8,128)}) custom-call(f32[2]{0:T(128)} %pad_maximum_fusion.2.scale_ref, f32[32,4352]{1,0:T(8,128)} %copy.95.left_ref, f32[32,4352]{1,0:T(8,128)} %copy.96.mid_ref, f32[32,4352]{1,0:T(8,128)} %copy.97.right_ref, f32[9,32,32]{2,1,0:T(8,128)} %w_ref.1, f32[32,4096]{1,0:T(8,128)} %bitcast.107), custom_call_target="tpu_custom_call" | custom-call | tf_op jit(solution)/shard_map/pallas_call | solution.py:159
  205.9 1.9 copy.103
  207.8 1.9 copy.104
  (77 shorter events, 22.1 us)
Async XLA Ops:
  7.2 15.7 %copy-start = (bf16[128,2048]{1,0:T(8,128)(2,1)S(1)}, bf16[128,2048]{1,0:T(8,128)(2,1)}, u32[]{:S(2)}) copy-start(bf16[128,2048]{1,0:T(8,128)(2,1)} %param.22) | copy-start | bytes 1572868
  7.2 102.8 %all-gather.5.cloned.1.call-start = ((), (), s32[]{:S(2)}) async-start(), calls=%async_computation | async-start | bytes 12976128 | tf_op jit(solution)/shard_map/all_gather | solution.py:97
  9.1 154.6 %all-gather.7.cloned.1.call-start = ((), (), s32[]{:S(2)}) async-start(), calls=%async_computation.1 | async-start | bytes 4456448 | tf_op jit(solution)/shard_map/all_gather | solution.py:114
  28.2 3.7 %copy-start.11 = (bf16[256,384]{1,0:T(8,128)(2,1)S(1)}, bf16[256,384]{1,0:T(8,128)(2,1)}, u32[]{:S(2)}) copy-start(bf16[256,384]{1,0:T(8,128)(2,1)} %param.23) | copy-start | bytes 589828
  28.2 27.5 %copy-start.8 = (f32[32,32,128]{2,1,0:T(8,128)S(1)}, f32[32,32,128]{2,1,0:T(8,128)}, u32[]{:S(2)}) copy-start(f32[32,32,128]{2,1,0:T(8,128)} %param.17) | copy-start | bytes 1572868
  123.5 4.7 %copy-start.7 = (f32[768,3072]{1,0:T(8,128)}, f32[768,3072]{1,0:T(8,128)S(1)}, u32[]{:S(2)}) copy-start(f32[768,3072]{1,0:T(8,128)S(1)} %fusion.48) | copy-start | bytes 28311556
  128.9 1.6 copy-start.2
  134.4 1.7 copy-start.4
  137.3 3.3 %copy-start.3 = (f32[96,8,8,128]{3,2,1,0:T(8,128)S(1)}, f32[96,8,8,128]{3,2,1,0:T(8,128)}, u32[]{:S(2)}) copy-start(f32[96,8,8,128]{3,2,1,0:T(8,128)} %copy-done.2) | copy-start | bytes 9437188
  137.3 3.3 %copy-start.12 = (f32[128]{0:T(128)S(1)}, f32[128]{0:T(128)}, u32[]{:S(2)}) copy-start(f32[128]{0:T(128)} %param.28) | copy-start | bytes 1540
  140.5 1.9 copy-start.5
  140.6 1.9 copy-start.13
  171.7 1.0 copy-start.10
  175.8 3.6 %copy-start.6 = (f32[32,32,128]{0,2,1:T(8,128)S(1)}, f32[32,32,128]{0,2,1:T(8,128)}, u32[]{:S(2)}) copy-start(f32[32,32,128]{0,2,1:T(8,128)} %copy.90) | copy-start | bytes 1572868
  179.4 6.7 %copy-start.9 = (f32[32,32,128]{2,1,0:T(8,128)S(1)}, f32[32,32,128]{2,1,0:T(8,128)}, u32[]{:S(2)}) copy-start(f32[32,32,128]{2,1,0:T(8,128)} %param.18) | copy-start | bytes 1572868
  180.2 7.0 %collective-permute-start = (f32[32,1,128]{0,2,1:T(8,128)S(1)}, f32[32,1,128]{0,2,1:T(8,128)S(1)}, u32[]{:S(2)}, u32[]{:S(2)}) collective-permute-start(f32[32,1,128]{0,2,1:T(8,128)S(1)} %get-tuple-element.13), channel_id=1, source_target_pairs={{0,1},{1,2},{2,3},{3,4},{4,5},{5,6},{6,7},{7,8},{8,9},{9,10},{10,1... | collective-permute-start | bytes 49160 | tf_op jit(solution)/shard_map/ppermute | solution.py:150
  183.4 5.6 %collective-permute-start.1 = (f32[32,1,128]{0,2,1:T(8,128)S(1)}, f32[32,1,128]{0,2,1:T(8,128)S(1)}, u32[]{:S(2)}, u32[]{:S(2)}) collective-permute-start(f32[32,1,128]{0,2,1:T(8,128)S(1)} %get-tuple-element.14), channel_id=1, source_target_pairs={{1,0},{2,1},{3,2},{4,3},{5,4},{6,5},{7,6},{8,7},{9,8},{10,9},{11,1... | collective-permute-start | bytes 49160 | tf_op jit(solution)/shard_map/ppermute | solution.py:151
  198.1 11.7 %copy-start.1 = (bf16[128,2048]{1,0:T(8,128)(2,1)S(1)}, bf16[128,2048]{1,0:T(8,128)(2,1)}, u32[]{:S(2)}) copy-start(bf16[128,2048]{1,0:T(8,128)(2,1)} %param.22) | copy-start | bytes 1572868
Sparse Core Ops, SparseCore 0:
  11.5 98.4 all-gather.4
  112.2 51.4 all-gather.6

commit v6 on v4

--- a/solution.py
+++ b/solution.py
@@ -184,7 +184,10 @@
     )
     chosen = jnp.take(tile_tokens, picked, axis=0)
     eps_chosen = denoise(chosen, *weights_all)
-    eps_back = jnp.take(eps_chosen, jnp.minimum(order_in, MAXOWN - 1), axis=0)
+    slot = jnp.minimum(order_in, MAXOWN - 1)[:, None, None]
+    eps_back = eps_chosen[MAXOWN - 1][None]
+    for index in range(MAXOWN - 2, -1, -1):
+        eps_back = jnp.where(slot == index, eps_chosen[index][None], eps_back)
     eps_tiles = jnp.where(cloudy[:, None, None] == 1, eps_back, jnp.zeros_like(eps_back))
     eps_latent = band_pixels(eps_tiles.astype(jnp.float32), tile_side, channels)
     cloud_cols = jnp.repeat(cloudy, band_rows) == 1

time: 203 us -> 202 us (level)
    broadcast_in_dim x0 -> x18, local copies, waits for them, and re-layouts: none -> 4.71 us  [the longest x16 4.49 us: on_device(): eps_back = jnp.where(slot == index, eps_chosen[index][None], eps_back)]
    unnamed x36 -> x38, local copies, waits for them, and re-layouts: 19.4 us -> 19.5 us
  transfers between devices with their start and end apart: 4 -> 4, of which waited for: 3 -> 3; matrix products, arithmetic and copies ran while one was open for 28% -> 29% of each run, Pallas kernels for 0% -> 0%
where the time goes in v6:
time: 202 us
  waiting for transfers between devices  69 us (34%)
  matrix products  34.3 us (17%)
  local copies, waits for them, and re-layouts  29.2 us (14%)
  other arithmetic  25 us (12%)
  blocking collectives  23 us (11%)
  between operations  15.6 us (8%)
  starting transfers between devices  5.43 us (3%)
    all_gather x1, waiting for transfers between devices, denoise(): lax.all_gather(share_of_part(jnp.concatenate([wq, wk, wv], axis=1)), ('ti...  55.4 us
    all_gather x1, blocking collectives, on_device(): modulation = lax.all_gather(local_mod, 'tile', axis=1, tiled=True)  23 us
    unnamed x38, local copies, waits for them, and re-layouts  19.5 us
    dot_general x1, matrix products, add_rows(): return jnp.dot(left, shard_rows, preferred_element_type=jnp.float32)  13.5 us
    all_gather x1, waiting for transfers between devices, denoise(): lax.all_gather(wo, 'tile', axis=1, tiled=True)  10.3 us
    dot_general x1, matrix products, denoise(): jnp.dot(mixed, lax.all_gather(wo, 'tile', axis=1, tiled=True), preferred_...  7.19 us
    dot_general x9, matrix products, on_device(): jnp.einsum('oc,chw->ohw', conv_w[3 * row_shift + col_shift], window, prec...  5.81 us
    convert_element_type x1, other arithmetic, denoise(): (layer_norm(hidden0) * (1.0 + scale_vec) + shift_vec).astype(jnp.bfloat16)  5.59 us
  transfers between devices with their start and end apart: 4, of which 3 were waited for; matrix products, arithmetic and copies ran while one was open for 29% of the time, Pallas kernels for 0%

profile of v6, /device:TPU:1, one launch (start us, length us, event | category | flops | bytes accessed | tf_op | source)
XLA Modules:
  0.0 201.6 jit_solution(9903168354687264281)
XLA Ops:
  7.2 1.9 fusion.53
  12.4 1.5 copy.84
  13.9 1.1 copy.85
  15.6 1.5 convert_element_type.57
  17.7 3.6 %fusion.86 = (f32[3,256]{1,0:T(4,128)S(1)}, f32[3,256,2048]{2,1,0:T(8,128)}) fusion(f32[256,2048]{1,0:T(8,128)S(1)} %convert_element_type.57, bf16[128,2048]{1,0:T(8,128)(2,1)S(1)} %copy-done, bf16[3,256,128]{2,1,0:T(8,128)(2,1)S(1)} %gather_fusion, pred[3]{0:T(512)(128)(4,1)S(1)} %compare_and_fusion), kind=kOutput, calls=%fused_computation.142 | convolution fusion | flops 405896448 | bytes 9112579 | tf_op jit(solution)/shard_map/dot_general | solution.py:98
  21.3 3.9 %multiply_reduce_fusion.1 = f32[3,256]{1,0:T(4,128)S(1)} fusion(f32[3,256,2048]{2,1,0:T(8,128)} %get-tuple-element.26, f32[3,256]{1,0:T(4,128)S(1)} %broadcast_multiply_fusion.1), kind=kLoop, calls=%fused_computation.12 | loop fusion | flops 4717824 | bytes 6297600 | tf_op jit(solution)/shard_map/reduce_sum | solution.py:43
  25.4 23.0 %all-gather.1 = f32[16,1,384]{2,1,0:T(1,128)S(1)} all-gather(f32[1,1,384]{2,1,0:T(1,128)S(1)} %convolution_bitcast_fusion), channel_id=2, replica_groups=mesh['grp'=2,'tile'=16] {'tile'}, dimensions={0}, use_global_device_ids=true | all-gather | bytes 26112 | tf_op jit(solution)/shard_map/all_gather | solution.py:160
  49.2 5.6 %fusion.4 = bf16[768,2048]{1,0:T(8,128)(2,1)} fusion(f32[3,256,2048]{2,1,0:T(8,128)} %get-tuple-element.26, f32[2048]{0:T(1024)S(1)} %bitcast.145, f32[2048]{0:T(1024)S(1)} %bitcast.144, f32[768]{0:T(1024)S(1)} %rsqrt.36, f32[768]{0:T(1024)S(1)} %div.60), kind=kLoop, calls=%fused_computation.7 | loop fusion | flops 7864320 | bytes 9459712 | tf_op jit(solution)/shard_map/convert_element_type | solution.py:102
  54.8 55.4 %all-gather.5.cloned.1.call-done = bf16[2048,3072]{1,0:T(8,128)(2,1)} async-done(((bf16[64,3072]{1,0:T(8,128)(2,1)}), bf16[2048,3072]{1,0:T(8,128)(2,1)}) %all-gather.5.cloned.1.call-update) | async-done | bytes 12582928 | tf_op jit(solution)/shard_map/all_gather | solution.py:108
  110.2 13.5 %fusion.89 = f32[768,3072]{1,0:T(8,128)S(1)} fusion(bf16[768,2048]{1,0:T(8,128)(2,1)} %fusion.4, bf16[2048,3072]{1,0:T(8,128)(2,1)} %all-gather.5.cloned.1.call-done), kind=kOutput, calls=%fused_computation.145 | convolution fusion | flops 9663676416 | bytes 25165824 | tf_op jit(solution)/shard_map/dot_general | solution.py:77
  123.7 2.8 %slice_bitcast_fusion.1 = (f32[96,8,8,128]{3,1,2,0:T(8,128)S(1)}, f32[96,8,8,128]{3,1,2,0:T(8,128)}) fusion(f32[768,3072]{1,0:T(8,128)S(1)} %fusion.89), kind=kLoop, calls=%fused_computation.28 | loop fusion | bytes 12582912
  126.5 1.9 copy-done.6
  129.1 1.6 copy-done.2
  130.8 0.9 fusion.12
  132.0 2.6 %copy.109 = f32[96,8,8,128]{3,2,1,0:T(8,128)S(1)} copy(f32[96,8,8,128]{3,1,2,0:T(8,128)} %get-tuple-element.15) | data formatting | bytes 6291456
  134.6 1.7 copy-done.4
  137.5 2.8 %fusion.20 = bf16[96,8,8,128]{3,1,2,0:T(8,128)(2,1)S(1)} fusion(f32[768,3072]{1,0:T(8,128)} %copy-done.6), kind=kLoop, calls=%fused_computation.37 | loop fusion | bytes 3145728
  140.8 1.0 fusion.14
  142.7 1.0 fusion.11
  143.7 1.0 fusion.24
  144.7 4.8 %fusion.87 = (f32[3,8,256]{2,1,0:T(8,128)S(1)}, f32[3,8,256,256]{2,3,1,0:T(8,128)S(1)}) fusion(f32[3,8,256,256]{2,3,1,0:T(8,128)S(1)} %fusion.24), kind=kOutput, calls=%fused_computation.143 | output fusion | flops 6291711 | bytes 12607488 | tf_op jit(solution)/shard_map/sub | solution.py:120
  149.5 2.0 %fusion.27 = bf16[3,256,8,128]{1,3,2,0:T(8,128)(2,1)} fusion(f32[3,8,256,256]{2,3,1,0:T(8,128)S(1)} %get-tuple-element.28, f32[3,8,256]{2,1,0:T(8,128)S(1)} %get-tuple-element.27, bf16[3,256,8,128]{3,2,1,0:T(8,128)(2,1)S(1)} %bitcast.138), kind=kOutput, calls=%fused_computation.44 | convolution fusion | flops 406585344 | bytes 9461760 | tf_op jit(solution)/shard_map/nhqk,nkhd->nqhd/dot_general | solution.py:122
  151.5 2.0 copy.94
  153.5 10.3 %all-gather.7.cloned.1.call-done = bf16[1024,2048]{1,0:T(8,128)(2,1)} async-done(((bf16[1024,128]{1,0:T(8,128)(2,1)}), bf16[1024,2048]{1,0:T(8,128)(2,1)}) %all-gather.7.cloned.1.call-update) | async-done | bytes 4194320 | tf_op jit(solution)/shard_map/all_gather | solution.py:125
  163.8 7.2 %fusion.88 = (f32[768]{0:T(1024)S(1)}, f32[768,2048]{1,0:T(8,128)S(1)}) fusion(bf16[1024,2048]{1,0:T(8,128)(2,1)} %all-gather.7.cloned.1.call-done, bf16[96,8,8,128]{3,2,1,0:T(8,128)(2,1)S(1)} %bitcast.139, f32[2048]{0:T(1024)S(1)} %bitcast.146, f32[3,256,2048]{2,1,0:T(8,128)} %get-tuple-element.26), kind=kOutput, calls=%fused_computation.144 | convolution fusion | flops 3225943296 | bytes 18361344 | tf_op jit(solution)/shard_map/dot_general | solution.py:124
  172.1 1.1 fusion.33
  178.0 3.2 %collective-permute-start = (f32[32,1,128]{2,0,1:T(8,128)S(1)}, f32[32,1,128]{2,0,1:T(8,128)S(1)}, u32[]{:S(2)}, u32[]{:S(2)}) collective-permute-start(f32[32,1,128]{2,0,1:T(8,128)S(1)} %get-tuple-element.16), channel_id=1, source_target_pairs={{0,1},{1,2},{2,3},{3,4},{4,5},{5,6},{6,7},{7,8},{8,9},{9,10},{10,1... | collective-permute-start | bytes 49160 | tf_op jit(solution)/shard_map/ppermute | solution.py:20
  181.2 2.2 %collective-permute-start.1 = (f32[32,1,128]{2,0,1:T(8,128)S(1)}, f32[32,1,128]{2,0,1:T(8,128)S(1)}, u32[]{:S(2)}, u32[]{:S(2)}) collective-permute-start(f32[32,1,128]{2,0,1:T(8,128)S(1)} %get-tuple-element.17), channel_id=1, source_target_pairs={{1,0},{2,1},{3,2},{4,3},{5,4},{6,5},{7,6},{8,7},{9,8},{10,9},{11,1... | collective-permute-start | bytes 49160 | tf_op jit(solution)/shard_map/ppermute | solution.py:23
  183.6 2.6 %collective-permute-done.1 = f32[32,1,128]{2,0,1:T(8,128)S(1)} collective-permute-done((f32[32,1,128]{2,0,1:T(8,128)S(1)}, f32[32,1,128]{2,0,1:T(8,128)S(1)}, u32[]{:S(2)}, u32[]{:S(2)}) %collective-permute-start.1) | collective-permute-done | bytes 16416 | tf_op jit(solution)/shard_map/ppermute | solution.py:23
  191.6 0.9 fusion.50
  192.5 1.1 copy.104
  193.6 1.1 copy.105
  (97 shorter events, 19.3 us)
Async XLA Ops:
  7.2 10.5 %copy-start = (bf16[128,2048]{1,0:T(8,128)(2,1)S(1)}, bf16[128,2048]{1,0:T(8,128)(2,1)}, u32[]{:S(2)}) copy-start(bf16[128,2048]{1,0:T(8,128)(2,1)} %param.22) | copy-start | bytes 1572868
  7.2 103.0 %all-gather.5.cloned.1.call-start = ((), (), s32[]{:S(2)}) async-start(), calls=%async_computation | async-start | bytes 12976128 | tf_op jit(solution)/shard_map/all_gather | solution.py:108
  9.1 154.7 %all-gather.7.cloned.1.call-start = ((), (), s32[]{:S(2)}) async-start(), calls=%async_computation.1 | async-start | bytes 4456448 | tf_op jit(solution)/shard_map/all_gather | solution.py:125
  21.3 3.9 %copy-start.11 = (bf16[256,384]{1,0:T(8,128)(2,1)S(1)}, bf16[256,384]{1,0:T(8,128)(2,1)}, u32[]{:S(2)}) copy-start(bf16[256,384]{1,0:T(8,128)(2,1)} %param.23) | copy-start | bytes 589828
  123.7 4.7 %copy-start.6 = (f32[768,3072]{1,0:T(8,128)}, f32[768,3072]{1,0:T(8,128)S(1)}, u32[]{:S(2)}) copy-start(f32[768,3072]{1,0:T(8,128)S(1)} %fusion.89) | copy-start | bytes 28311556
  129.1 1.6 copy-start.2
  134.6 1.7 copy-start.4
  137.5 3.3 %copy-start.3 = (f32[96,8,8,128]{3,2,1,0:T(8,128)S(1)}, f32[96,8,8,128]{3,2,1,0:T(8,128)}, u32[]{:S(2)}) copy-start(f32[96,8,8,128]{3,2,1,0:T(8,128)} %copy-done.2) | copy-start | bytes 9437188
  137.5 3.3 %copy-start.13 = (f32[128]{0:T(128)S(1)}, f32[128]{0:T(128)}, u32[]{:S(2)}) copy-start(f32[128]{0:T(128)} %param.28) | copy-start | bytes 1540
  140.7 1.9 copy-start.5
  140.7 1.9 copy-start.14
  171.0 1.0 copy-start.10
  174.9 2.4 %copy-start.7 = (f32[32,32,128]{2,1,0:T(8,128)S(1)}, f32[32,32,128]{2,1,0:T(8,128)}, u32[]{:S(2)}) copy-start(f32[32,32,128]{2,1,0:T(8,128)} %param.16) | copy-start | bytes 1572868
  174.9 2.4 %copy-start.8 = (f32[32,32,128]{2,1,0:T(8,128)S(1)}, f32[32,32,128]{2,1,0:T(8,128)}, u32[]{:S(2)}) copy-start(f32[32,32,128]{2,1,0:T(8,128)} %param.17) | copy-start | bytes 1572868
  176.3 10.3 %copy-start.12 = (f32[9,32,32]{2,1,0:T(8,128)S(1)}, f32[9,32,32]{2,1,0:T(8,128)}, u32[]{:S(2)}) copy-start(f32[9,32,32]{2,1,0:T(8,128)} %param.31) | copy-start | bytes 110596
  178.0 5.6 %collective-permute-start = (f32[32,1,128]{2,0,1:T(8,128)S(1)}, f32[32,1,128]{2,0,1:T(8,128)S(1)}, u32[]{:S(2)}, u32[]{:S(2)}) collective-permute-start(f32[32,1,128]{2,0,1:T(8,128)S(1)} %get-tuple-element.16), channel_id=1, source_target_pairs={{0,1},{1,2},{2,3},{3,4},{4,5},{5,6},{6,7},{7,8},{8,9},{9,10},{10,1... | collective-permute-start | bytes 49160 | tf_op jit(solution)/shard_map/ppermute | solution.py:20
  181.2 5.1 %collective-permute-start.1 = (f32[32,1,128]{2,0,1:T(8,128)S(1)}, f32[32,1,128]{2,0,1:T(8,128)S(1)}, u32[]{:S(2)}, u32[]{:S(2)}) collective-permute-start(f32[32,1,128]{2,0,1:T(8,128)S(1)} %get-tuple-element.17), channel_id=1, source_target_pairs={{1,0},{2,1},{3,2},{4,3},{5,4},{6,5},{7,6},{8,7},{9,8},{10,9},{11,1... | collective-permute-start | bytes 49160 | tf_op jit(solution)/shard_map/ppermute | solution.py:23
  189.2 2.5 %copy-start.9 = (f32[32,32,128]{2,1,0:T(8,128)S(1)}, f32[32,32,128]{2,1,0:T(8,128)}, u32[]{:S(2)}) copy-start(f32[32,32,128]{2,1,0:T(8,128)} %param.18) | copy-start | bytes 1572868
  191.0 3.7 %copy-start.1 = (bf16[128,2048]{1,0:T(8,128)(2,1)S(1)}, bf16[128,2048]{1,0:T(8,128)(2,1)}, u32[]{:S(2)}) copy-start(bf16[128,2048]{1,0:T(8,128)(2,1)} %param.22) | copy-start | bytes 1572868
Sparse Core Ops, SparseCore 0:
  11.5 98.6 all-gather.4
  112.3 51.4 all-gather.6

commit v7 on v4

--- a/solution.py
+++ b/solution.py
@@ -184,9 +184,14 @@
     )
     chosen = jnp.take(tile_tokens, picked, axis=0)
     eps_chosen = denoise(chosen, *weights_all)
-    eps_back = jnp.take(eps_chosen, jnp.minimum(order_in, MAXOWN - 1), axis=0)
-    eps_tiles = jnp.where(cloudy[:, None, None] == 1, eps_back, jnp.zeros_like(eps_back))
-    eps_latent = band_pixels(eps_tiles.astype(jnp.float32), tile_side, channels)
+    slot = jnp.minimum(order_in, MAXOWN - 1)
+    eps_tiles = []
+    for tile in range(tiles_here):
+        tile_eps = eps_chosen[MAXOWN - 1]
+        for index in range(MAXOWN - 2, -1, -1):
+            tile_eps = jnp.where(slot[tile] == index, eps_chosen[index], tile_eps)
+        eps_tiles.append(tile_eps)
+    eps_latent = band_pixels(jnp.stack(eps_tiles).astype(jnp.float32), tile_side, channels)
     cloud_cols = jnp.repeat(cloudy, band_rows) == 1
     raw_estimate = jnp.where(
         cloud_cols[None, None, :], (latent - sin_now * eps_latent) / cos_now, observed

time: 203 us -> 203 us (level)
  waiting for transfers between devices: 70 us -> 63 us
  between operations: 15.5 us -> 20.6 us
    all_gather x1, waiting for transfers between devices: 56 us -> 49.1 us  [denoise(): lax.all_gather(share_of_part(jnp.concatenate([wq, wk, wv], axis=1)), ('ti...]
  transfers between devices with their start and end apart: 4 -> 4, of which waited for: 3 -> 3; matrix products, arithmetic and copies ran while one was open for 28% -> 29% of each run, Pallas kernels for 0% -> 0%
where the time goes in v7:
time: 203 us
  waiting for transfers between devices  63 us (31%)
  matrix products  34.4 us (17%)
  other arithmetic  28.9 us (14%)
  local copies, waits for them, and re-layouts  27 us (13%)
  blocking collectives  23.5 us (12%)
  between operations  20.6 us (10%)
  starting transfers between devices  5.16 us (3%)
    all_gather x1, waiting for transfers between devices, denoise(): lax.all_gather(share_of_part(jnp.concatenate([wq, wk, wv], axis=1)), ('ti...  49.1 us
    all_gather x1, blocking collectives, on_device(): modulation = lax.all_gather(local_mod, 'tile', axis=1, tiled=True)  23.5 us
    unnamed x36, local copies, waits for them, and re-layouts  19.5 us
    dot_general x1, matrix products, add_rows(): return jnp.dot(left, shard_rows, preferred_element_type=jnp.float32)  13.5 us
    all_gather x1, waiting for transfers between devices, denoise(): lax.all_gather(wo, 'tile', axis=1, tiled=True)  10.3 us
    dot_general x1, matrix products, denoise(): jnp.dot(mixed, lax.all_gather(wo, 'tile', axis=1, tiled=True), preferred_...  7.19 us
    dot_general x9, matrix products, on_device(): jnp.einsum('oc,chw->ohw', conv_w[3 * row_shift + col_shift], window, prec...  5.81 us
    convert_element_type x1, other arithmetic, denoise(): (layer_norm(hidden0) * (1.0 + scale_vec) + shift_vec).astype(jnp.bfloat16)  5.64 us
  transfers between devices with their start and end apart: 4, of which 3 were waited for; matrix products, arithmetic and copies ran while one was open for 29% of the time, Pallas kernels for 0%

profile of v7, /device:TPU:1, one launch (start us, length us, event | category | flops | bytes accessed | tf_op | source)
XLA Modules:
  0.0 202.6 jit_solution(2164988827635296202)
XLA Ops:
  7.2 1.9 fusion.53
  18.8 1.5 copy.79
  20.3 1.1 copy.80
  22.0 1.5 convert_element_type.55
  24.1 3.6 %fusion.86 = (f32[3,256]{1,0:T(4,128)S(1)}, f32[3,256,2048]{2,1,0:T(8,128)}) fusion(f32[256,2048]{1,0:T(8,128)S(1)} %convert_element_type.55, bf16[128,2048]{1,0:T(8,128)(2,1)S(1)} %copy-done, bf16[3,256,128]{2,1,0:T(8,128)(2,1)S(1)} %gather_fusion, pred[3]{0:T(512)(128)(4,1)S(1)} %compare_and_fusion), kind=kOutput, calls=%fused_computation.147 | convolution fusion | flops 405896448 | bytes 9112579 | tf_op jit(solution)/shard_map/dot_general | solution.py:98
  27.7 3.6 %multiply_reduce_fusion.1 = f32[3,256]{1,0:T(4,128)S(1)} fusion(f32[3,256,2048]{2,1,0:T(8,128)} %get-tuple-element.29, f32[3,256]{1,0:T(4,128)S(1)} %broadcast_multiply_fusion.1), kind=kLoop, calls=%fused_computation.12 | loop fusion | flops 4717824 | bytes 6297600 | tf_op jit(solution)/shard_map/reduce_sum | solution.py:43
  31.5 23.5 %all-gather.1 = f32[16,1,384]{2,1,0:T(1,128)S(1)} all-gather(f32[1,1,384]{2,1,0:T(1,128)S(1)} %convolution_bitcast_fusion), channel_id=2, replica_groups=mesh['grp'=2,'tile'=16] {'tile'}, dimensions={0}, use_global_device_ids=true | all-gather | bytes 26112 | tf_op jit(solution)/shard_map/all_gather | solution.py:160
  55.2 5.6 %fusion.4 = bf16[768,2048]{1,0:T(8,128)(2,1)} fusion(f32[3,256,2048]{2,1,0:T(8,128)} %get-tuple-element.29, f32[2048]{0:T(1024)S(1)} %bitcast.145, f32[2048]{0:T(1024)S(1)} %bitcast.144, f32[768]{0:T(1024)S(1)} %rsqrt.36, f32[768]{0:T(1024)S(1)} %div.60), kind=kLoop, calls=%fused_computation.7 | loop fusion | flops 7864320 | bytes 9459712 | tf_op jit(solution)/shard_map/convert_element_type | solution.py:102
  60.9 49.1 %all-gather.5.cloned.1.call-done = bf16[2048,3072]{1,0:T(8,128)(2,1)} async-done(((bf16[64,3072]{1,0:T(8,128)(2,1)}), bf16[2048,3072]{1,0:T(8,128)(2,1)}) %all-gather.5.cloned.1.call-update) | async-done | bytes 12582928 | tf_op jit(solution)/shard_map/all_gather | solution.py:108
  110.0 13.5 %fusion.89 = f32[768,3072]{1,0:T(8,128)S(1)} fusion(bf16[768,2048]{1,0:T(8,128)(2,1)} %fusion.4, bf16[2048,3072]{1,0:T(8,128)(2,1)} %all-gather.5.cloned.1.call-done), kind=kOutput, calls=%fused_computation.150 | convolution fusion | flops 9663676416 | bytes 25165824 | tf_op jit(solution)/shard_map/dot_general | solution.py:77
  123.5 2.8 %slice_bitcast_fusion.1 = (f32[96,8,8,128]{3,1,2,0:T(8,128)S(1)}, f32[96,8,8,128]{3,1,2,0:T(8,128)}) fusion(f32[768,3072]{1,0:T(8,128)S(1)} %fusion.89), kind=kLoop, calls=%fused_computation.28 | loop fusion | bytes 12582912
  126.3 1.9 copy-done.6
  128.9 1.6 copy-done.2
  131.8 2.6 %copy.104 = f32[96,8,8,128]{3,2,1,0:T(8,128)S(1)} copy(f32[96,8,8,128]{3,1,2,0:T(8,128)} %get-tuple-element.15) | data formatting | bytes 6291456
  134.4 1.7 copy-done.4
  137.3 2.8 %fusion.20 = bf16[96,8,8,128]{3,1,2,0:T(8,128)(2,1)S(1)} fusion(f32[768,3072]{1,0:T(8,128)} %copy-done.6), kind=kLoop, calls=%fused_computation.38 | loop fusion | bytes 3145728
  140.6 1.0 fusion.14
  142.5 1.0 fusion.11
  143.5 1.0 fusion.24
  144.5 4.8 %fusion.87 = (f32[3,8,256]{2,1,0:T(8,128)S(1)}, f32[3,8,256,256]{2,3,1,0:T(8,128)S(1)}) fusion(f32[3,8,256,256]{2,3,1,0:T(8,128)S(1)} %fusion.24), kind=kOutput, calls=%fused_computation.148 | output fusion | flops 6291711 | bytes 12607488 | tf_op jit(solution)/shard_map/sub | solution.py:120
  149.3 2.0 fusion.27
  151.3 2.0 copy.89
  153.3 10.3 %all-gather.7.cloned.1.call-done = bf16[1024,2048]{1,0:T(8,128)(2,1)} async-done(((bf16[1024,128]{1,0:T(8,128)(2,1)}), bf16[1024,2048]{1,0:T(8,128)(2,1)}) %all-gather.7.cloned.1.call-update) | async-done | bytes 4194320 | tf_op jit(solution)/shard_map/all_gather | solution.py:125
  163.6 7.2 %fusion.88 = (f32[768]{0:T(1024)S(1)}, f32[768,2048]{1,0:T(8,128)S(1)}) fusion(bf16[1024,2048]{1,0:T(8,128)(2,1)} %all-gather.7.cloned.1.call-done, bf16[96,8,8,128]{3,2,1,0:T(8,128)(2,1)S(1)} %bitcast.142, f32[2048]{0:T(1024)S(1)} %bitcast.146, f32[3,256,2048]{2,1,0:T(8,128)} %get-tuple-element.29), kind=kOutput, calls=%fused_computation.149 | convolution fusion | flops 3225943296 | bytes 18361344 | tf_op jit(solution)/shard_map/dot_general | solution.py:124
  171.9 1.1 fusion.33
  174.4 2.4 %convert_multiply_fusion = f32[4,16,16,2,2,32]{5,4,2,0,3,1:T(2,128)S(1)} fusion(f32[]{:T(128)S(6)} %sin.9, bf16[1,16,16,2,2,32]{5,4,3,2,1,0:T(2,128)(2,1)S(1)} %stack.18, bf16[1,16,16,2,2,32]{5,4,3,2,1,0:T(2,128)(2,1)} %stack.17, bf16[1,16,16,2,2,32]{5,4,3,2,1,0:T(2,128)(2,1)S(1)} %stack.16, bf16[1,16,16,2,2,32]{5,4,3,2,1,0:T(2,128)(2,1)S(1)} %stack.15), kind=kLoop, calls=%fused_computation.34 | loop fusion | flops 655360 | bytes 786436 | tf_op jit(solution)/shard_map/mul | solution.py:197
  177.4 1.6 copy_select_fusion
  179.0 3.2 %collective-permute-start = (f32[32,1,128]{2,0,1:T(8,128)S(1)}, f32[32,1,128]{2,0,1:T(8,128)S(1)}, u32[]{:S(2)}, u32[]{:S(2)}) collective-permute-start(f32[32,1,128]{2,0,1:T(8,128)S(1)} %get-tuple-element.16), channel_id=1, source_target_pairs={{0,1},{1,2},{2,3},{3,4},{4,5},{5,6},{6,7},{7,8},{8,9},{9,10},{10,1... | collective-permute-start | bytes 49160 | tf_op jit(solution)/shard_map/ppermute | solution.py:20
  182.2 1.9 collective-permute-start.1
  184.4 2.9 %collective-permute-done.1 = f32[32,1,128]{2,0,1:T(8,128)S(1)} collective-permute-done((f32[32,1,128]{2,0,1:T(8,128)S(1)}, f32[32,1,128]{2,0,1:T(8,128)S(1)}, u32[]{:S(2)}, u32[]{:S(2)}) %collective-permute-start.1) | collective-permute-done | bytes 16416 | tf_op jit(solution)/shard_map/ppermute | solution.py:23
  193.6 1.1 copy.98
  194.7 1.1 copy.99
  (85 shorter events, 18.9 us)
Async XLA Ops:
  7.2 16.9 %copy-start = (bf16[128,2048]{1,0:T(8,128)(2,1)S(1)}, bf16[128,2048]{1,0:T(8,128)(2,1)}, u32[]{:S(2)}) copy-start(bf16[128,2048]{1,0:T(8,128)(2,1)} %param.22) | copy-start | bytes 1572868
  7.2 102.8 %all-gather.5.cloned.1.call-start = ((), (), s32[]{:S(2)}) async-start(), calls=%async_computation | async-start | bytes 12976128 | tf_op jit(solution)/shard_map/all_gather | solution.py:108
  9.1 154.5 %all-gather.7.cloned.1.call-start = ((), (), s32[]{:S(2)}) async-start(), calls=%async_computation.1 | async-start | bytes 4456448 | tf_op jit(solution)/shard_map/all_gather | solution.py:125
  27.7 3.7 %copy-start.10 = (bf16[256,384]{1,0:T(8,128)(2,1)S(1)}, bf16[256,384]{1,0:T(8,128)(2,1)}, u32[]{:S(2)}) copy-start(bf16[256,384]{1,0:T(8,128)(2,1)} %param.23) | copy-start | bytes 589828
  123.5 4.7 %copy-start.6 = (f32[768,3072]{1,0:T(8,128)}, f32[768,3072]{1,0:T(8,128)S(1)}, u32[]{:S(2)}) copy-start(f32[768,3072]{1,0:T(8,128)S(1)} %fusion.89) | copy-start | bytes 28311556
  128.9 1.6 copy-start.2
  134.4 1.7 copy-start.4
  137.3 3.3 %copy-start.3 = (f32[96,8,8,128]{3,2,1,0:T(8,128)S(1)}, f32[96,8,8,128]{3,2,1,0:T(8,128)}, u32[]{:S(2)}) copy-start(f32[96,8,8,128]{3,2,1,0:T(8,128)} %copy-done.2) | copy-start | bytes 9437188
  137.3 3.3 %copy-start.12 = (f32[128]{0:T(128)S(1)}, f32[128]{0:T(128)}, u32[]{:S(2)}) copy-start(f32[128]{0:T(128)} %param.28) | copy-start | bytes 1540
  140.5 1.9 copy-start.5
  140.5 1.9 copy-start.13
  170.8 1.0 copy-start.9
  173.5 3.9 %copy-start.7 = (f32[32,32,128]{2,1,0:T(8,128)S(1)}, f32[32,32,128]{2,1,0:T(8,128)}, u32[]{:S(2)}) copy-start(f32[32,32,128]{2,1,0:T(8,128)} %param.16) | copy-start | bytes 1572868
  176.8 10.8 %copy-start.11 = (f32[9,32,32]{2,1,0:T(8,128)S(1)}, f32[9,32,32]{2,1,0:T(8,128)}, u32[]{:S(2)}) copy-start(f32[9,32,32]{2,1,0:T(8,128)} %param.31) | copy-start | bytes 110596
  179.0 5.3 %collective-permute-start = (f32[32,1,128]{2,0,1:T(8,128)S(1)}, f32[32,1,128]{2,0,1:T(8,128)S(1)}, u32[]{:S(2)}, u32[]{:S(2)}) collective-permute-start(f32[32,1,128]{2,0,1:T(8,128)S(1)} %get-tuple-element.16), channel_id=1, source_target_pairs={{0,1},{1,2},{2,3},{3,4},{4,5},{5,6},{6,7},{7,8},{8,9},{9,10},{10,1... | collective-permute-start | bytes 49160 | tf_op jit(solution)/shard_map/ppermute | solution.py:20
  182.2 5.1 %collective-permute-start.1 = (f32[32,1,128]{2,0,1:T(8,128)S(1)}, f32[32,1,128]{2,0,1:T(8,128)S(1)}, u32[]{:S(2)}, u32[]{:S(2)}) collective-permute-start(f32[32,1,128]{2,0,1:T(8,128)S(1)} %get-tuple-element.17), channel_id=1, source_target_pairs={{1,0},{2,1},{3,2},{4,3},{5,4},{6,5},{7,6},{8,7},{9,8},{10,9},{11,1... | collective-permute-start | bytes 49160 | tf_op jit(solution)/shard_map/ppermute | solution.py:23
  190.2 2.5 %copy-start.8 = (f32[32,32,128]{2,1,0:T(8,128)S(1)}, f32[32,32,128]{2,1,0:T(8,128)}, u32[]{:S(2)}) copy-start(f32[32,32,128]{2,1,0:T(8,128)} %param.18) | copy-start | bytes 1572868
  192.1 3.7 %copy-start.1 = (bf16[128,2048]{1,0:T(8,128)(2,1)S(1)}, bf16[128,2048]{1,0:T(8,128)(2,1)}, u32[]{:S(2)}) copy-start(bf16[128,2048]{1,0:T(8,128)(2,1)} %param.22) | copy-start | bytes 1572868
Sparse Core Ops, SparseCore 0:
  11.5 98.4 all-gather.4
  112.1 51.4 all-gather.6

commit v8 on v7

--- a/solution.py
+++ b/solution.py
@@ -184,14 +184,17 @@
     )
     chosen = jnp.take(tile_tokens, picked, axis=0)
     eps_chosen = denoise(chosen, *weights_all)
+    slot_px = band_pixels(eps_chosen.astype(jnp.float32), tile_side, channels)
     slot = jnp.minimum(order_in, MAXOWN - 1)
-    eps_tiles = []
+    tile_px = tile_side * PATCH
+    blocks = [slot_px[:, :, index * tile_px : (index + 1) * tile_px] for index in range(MAXOWN)]
+    columns = []
     for tile in range(tiles_here):
-        tile_eps = eps_chosen[MAXOWN - 1]
+        block = blocks[MAXOWN - 1]
         for index in range(MAXOWN - 2, -1, -1):
-            tile_eps = jnp.where(slot[tile] == index, eps_chosen[index], tile_eps)
-        eps_tiles.append(tile_eps)
-    eps_latent = band_pixels(jnp.stack(eps_tiles).astype(jnp.float32), tile_side, channels)
+            block = jnp.where(slot[tile] == index, blocks[index], block)
+        columns.append(block)
+    eps_latent = jnp.concatenate(columns, axis=2)
     cloud_cols = jnp.repeat(cloudy, band_rows) == 1
     raw_estimate = jnp.where(
         cloud_cols[None, None, :], (latent - sin_now * eps_latent) / cos_now, observed

time: 203 us -> 202 us (level)
  other arithmetic: 28.9 us -> 25.9 us
    mul x1 -> x0, other arithmetic: 2.41 us -> none  [on_device(): sin_now * eps_latent]
    reshape x0 -> x2, local copies, waits for them, and re-layouts: none -> 2.1 us  [band_pixels(): jnp.transpose(shaped, (5, 1, 3, 0, 2, 4))]
    unnamed x36 -> x41, local copies, waits for them, and re-layouts: 19.5 us -> 20.5 us
where the time goes in v8:
time: 202 us; the launch traced here: 201 us
  waiting for transfers between devices  63.1 us (31%)
  matrix products  34.3 us (17%)
  local copies, waits for them, and re-layouts  28.4 us (14%)
  other arithmetic  25.9 us (13%)
  blocking collectives  23.5 us (12%)
  between operations  20.6 us (10%)
  starting transfers between devices  5.17 us (3%)
    all_gather x1, waiting for transfers between devices, denoise(): lax.all_gather(share_of_part(jnp.concatenate([wq, wk, wv], axis=1)), ('ti...  49.1 us
    all_gather x1, blocking collectives, on_device(): modulation = lax.all_gather(local_mod, 'tile', axis=1, tiled=True)  23.5 us
    unnamed x41, local copies, waits for them, and re-layouts  20.5 us
    dot_general x1, matrix products, add_rows(): return jnp.dot(left, shard_rows, preferred_element_type=jnp.float32)  13.5 us
    all_gather x1, waiting for transfers between devices, denoise(): lax.all_gather(wo, 'tile', axis=1, tiled=True)  10.4 us
    dot_general x1, matrix products, denoise(): jnp.dot(mixed, lax.all_gather(wo, 'tile', axis=1, tiled=True), preferred_...  7.19 us
    dot_general x9, matrix products, on_device(): jnp.einsum('oc,chw->ohw', conv_w[3 * row_shift + col_shift], window, prec...  5.81 us
    convert_element_type x1, other arithmetic, denoise(): (layer_norm(hidden0) * (1.0 + scale_vec) + shift_vec).astype(jnp.bfloat16)  5.63 us
  transfers between devices with their start and end apart: 4, of which 3 were waited for; matrix products, arithmetic and copies ran while one was open for 29% of the time, Pallas kernels for 0%

profile of v8, /device:TPU:1, one launch (start us, length us, event | category | flops | bytes accessed | tf_op | source)
XLA Modules:
  0.0 201.0 jit_solution(2919327206144007510)
XLA Ops:
  7.2 1.9 fusion.56
  18.8 1.5 copy.76
  20.3 1.1 copy.77
  22.0 1.5 convert_element_type.56
  24.1 3.6 %fusion.90 = (f32[3,256]{1,0:T(4,128)S(1)}, f32[3,256,2048]{2,1,0:T(8,128)}) fusion(f32[256,2048]{1,0:T(8,128)S(1)} %convert_element_type.56, bf16[128,2048]{1,0:T(8,128)(2,1)S(1)} %copy-done, bf16[3,256,128]{2,1,0:T(8,128)(2,1)S(1)} %gather_fusion, pred[3]{0:T(512)(128)(4,1)S(1)} %compare_and_fusion), kind=kOutput, calls=%fused_computation.148 | convolution fusion | flops 405896448 | bytes 9112579 | tf_op jit(solution)/shard_map/dot_general | solution.py:98
  27.7 3.6 %multiply_reduce_fusion.1 = f32[3,256]{1,0:T(4,128)S(1)} fusion(f32[3,256,2048]{2,1,0:T(8,128)} %get-tuple-element.33, f32[3,256]{1,0:T(4,128)S(1)} %broadcast_multiply_fusion.1), kind=kLoop, calls=%fused_computation.12 | loop fusion | flops 4717824 | bytes 6297600 | tf_op jit(solution)/shard_map/reduce_sum | solution.py:43
  31.6 23.5 %all-gather.1 = f32[16,1,384]{2,1,0:T(1,128)S(1)} all-gather(f32[1,1,384]{2,1,0:T(1,128)S(1)} %convolution_bitcast_fusion), channel_id=2, replica_groups=mesh['grp'=2,'tile'=16] {'tile'}, dimensions={0}, use_global_device_ids=true | all-gather | bytes 26112 | tf_op jit(solution)/shard_map/all_gather | solution.py:160
  55.3 5.6 %fusion.4 = bf16[768,2048]{1,0:T(8,128)(2,1)} fusion(f32[3,256,2048]{2,1,0:T(8,128)} %get-tuple-element.33, f32[2048]{0:T(1024)S(1)} %bitcast.145, f32[2048]{0:T(1024)S(1)} %bitcast.144, f32[768]{0:T(1024)S(1)} %rsqrt.36, f32[768]{0:T(1024)S(1)} %div.60), kind=kLoop, calls=%fused_computation.7 | loop fusion | flops 7864320 | bytes 9459712 | tf_op jit(solution)/shard_map/convert_element_type | solution.py:102
  60.9 49.1 %all-gather.5.cloned.1.call-done = bf16[2048,3072]{1,0:T(8,128)(2,1)} async-done(((bf16[64,3072]{1,0:T(8,128)(2,1)}), bf16[2048,3072]{1,0:T(8,128)(2,1)}) %all-gather.5.cloned.1.call-update) | async-done | bytes 12582928 | tf_op jit(solution)/shard_map/all_gather | solution.py:108
  110.0 13.5 %fusion.93 = f32[768,3072]{1,0:T(8,128)S(1)} fusion(bf16[768,2048]{1,0:T(8,128)(2,1)} %fusion.4, bf16[2048,3072]{1,0:T(8,128)(2,1)} %all-gather.5.cloned.1.call-done), kind=kOutput, calls=%fused_computation.151 | convolution fusion | flops 9663676416 | bytes 25165824 | tf_op jit(solution)/shard_map/dot_general | solution.py:77
  123.4 2.8 %slice_bitcast_fusion.1 = (f32[96,8,8,128]{3,1,2,0:T(8,128)S(1)}, f32[96,8,8,128]{3,1,2,0:T(8,128)}) fusion(f32[768,3072]{1,0:T(8,128)S(1)} %fusion.93), kind=kLoop, calls=%fused_computation.28 | loop fusion | bytes 12582912
  126.2 1.9 copy-done.6
  128.8 1.6 copy-done.2
  130.5 0.9 fusion.12
  131.7 2.6 %copy.102 = f32[96,8,8,128]{3,2,1,0:T(8,128)S(1)} copy(f32[96,8,8,128]{3,1,2,0:T(8,128)} %get-tuple-element.15) | data formatting | bytes 6291456
  134.3 1.7 copy-done.4
  137.2 2.7 %fusion.20 = bf16[96,8,8,128]{3,1,2,0:T(8,128)(2,1)S(1)} fusion(f32[768,3072]{1,0:T(8,128)} %copy-done.6), kind=kLoop, calls=%fused_computation.37 | loop fusion | bytes 3145728
  140.5 1.0 fusion.14
  142.4 1.0 fusion.11
  143.4 1.0 fusion.24
  144.4 4.8 %fusion.91 = (f32[3,8,256]{2,1,0:T(8,128)S(1)}, f32[3,8,256,256]{2,3,1,0:T(8,128)S(1)}) fusion(f32[3,8,256,256]{2,3,1,0:T(8,128)S(1)} %fusion.24), kind=kOutput, calls=%fused_computation.149 | output fusion | flops 6291711 | bytes 12607488 | tf_op jit(solution)/shard_map/sub | solution.py:120
  149.2 2.0 %fusion.27 = bf16[3,256,8,128]{1,3,2,0:T(8,128)(2,1)} fusion(f32[3,8,256,256]{2,3,1,0:T(8,128)S(1)} %get-tuple-element.35, f32[3,8,256]{2,1,0:T(8,128)S(1)} %get-tuple-element.34, bf16[3,256,8,128]{3,2,1,0:T(8,128)(2,1)S(1)} %bitcast.141), kind=kOutput, calls=%fused_computation.44 | convolution fusion | flops 406585344 | bytes 9461760 | tf_op jit(solution)/shard_map/nhqk,nkhd->nqhd/dot_general | solution.py:122
  151.2 2.0 copy.86
  153.2 10.4 %all-gather.7.cloned.1.call-done = bf16[1024,2048]{1,0:T(8,128)(2,1)} async-done(((bf16[1024,128]{1,0:T(8,128)(2,1)}), bf16[1024,2048]{1,0:T(8,128)(2,1)}) %all-gather.7.cloned.1.call-update) | async-done | bytes 4194320 | tf_op jit(solution)/shard_map/all_gather | solution.py:125
  163.6 7.2 %fusion.92 = (f32[768]{0:T(1024)S(1)}, f32[768,2048]{1,0:T(8,128)S(1)}) fusion(bf16[1024,2048]{1,0:T(8,128)(2,1)} %all-gather.7.cloned.1.call-done, bf16[96,8,8,128]{3,2,1,0:T(8,128)(2,1)S(1)} %bitcast.142, f32[2048]{0:T(1024)S(1)} %bitcast.146, f32[3,256,2048]{2,1,0:T(8,128)} %get-tuple-element.33), kind=kOutput, calls=%fused_computation.150 | convolution fusion | flops 3225943296 | bytes 18361344 | tf_op jit(solution)/shard_map/dot_general | solution.py:124
  171.9 1.1 fusion.34
  172.9 1.3 reshape.261
  177.4 3.2 %collective-permute-start = (f32[32,1,128]{2,0,1:T(8,128)S(1)}, f32[32,1,128]{2,0,1:T(8,128)S(1)}, u32[]{:S(2)}, u32[]{:S(2)}) collective-permute-start(f32[32,1,128]{2,0,1:T(8,128)S(1)} %get-tuple-element.23), channel_id=1, source_target_pairs={{0,1},{1,2},{2,3},{3,4},{4,5},{5,6},{6,7},{7,8},{8,9},{9,10},{10,1... | collective-permute-start | bytes 49160 | tf_op jit(solution)/shard_map/ppermute | solution.py:20
  180.6 1.9 collective-permute-start.1
  182.8 2.9 %collective-permute-done.1 = f32[32,1,128]{2,0,1:T(8,128)S(1)} collective-permute-done((f32[32,1,128]{2,0,1:T(8,128)S(1)}, f32[32,1,128]{2,0,1:T(8,128)S(1)}, u32[]{:S(2)}, u32[]{:S(2)}) %collective-permute-start.1) | collective-permute-done | bytes 16416 | tf_op jit(solution)/shard_map/ppermute | solution.py:23
  191.9 1.1 copy.94
  193.0 1.1 copy.95
  (86 shorter events, 19.2 us)
Async XLA Ops:
  7.2 16.9 %copy-start = (bf16[128,2048]{1,0:T(8,128)(2,1)S(1)}, bf16[128,2048]{1,0:T(8,128)(2,1)}, u32[]{:S(2)}) copy-start(bf16[128,2048]{1,0:T(8,128)(2,1)} %param.22) | copy-start | bytes 1572868
  7.2 102.8 %all-gather.5.cloned.1.call-start = ((), (), s32[]{:S(2)}) async-start(), calls=%async_computation | async-start | bytes 12976128 | tf_op jit(solution)/shard_map/all_gather | solution.py:108
  9.1 154.5 %all-gather.7.cloned.1.call-start = ((), (), s32[]{:S(2)}) async-start(), calls=%async_computation.1 | async-start | bytes 4456448 | tf_op jit(solution)/shard_map/all_gather | solution.py:125
  27.7 3.7 %copy-start.11 = (bf16[256,384]{1,0:T(8,128)(2,1)S(1)}, bf16[256,384]{1,0:T(8,128)(2,1)}, u32[]{:S(2)}) copy-start(bf16[256,384]{1,0:T(8,128)(2,1)} %param.23) | copy-start | bytes 589828
  123.4 4.7 %copy-start.6 = (f32[768,3072]{1,0:T(8,128)}, f32[768,3072]{1,0:T(8,128)S(1)}, u32[]{:S(2)}) copy-start(f32[768,3072]{1,0:T(8,128)S(1)} %fusion.93) | copy-start | bytes 28311556
  128.8 1.6 copy-start.2
  134.3 1.7 copy-start.4
  137.2 3.3 %copy-start.3 = (f32[96,8,8,128]{3,2,1,0:T(8,128)S(1)}, f32[96,8,8,128]{3,2,1,0:T(8,128)}, u32[]{:S(2)}) copy-start(f32[96,8,8,128]{3,2,1,0:T(8,128)} %copy-done.2) | copy-start | bytes 9437188
  137.2 3.3 %copy-start.13 = (f32[128]{0:T(128)S(1)}, f32[128]{0:T(128)}, u32[]{:S(2)}) copy-start(f32[128]{0:T(128)} %param.28) | copy-start | bytes 1540
  140.4 1.9 copy-start.5
  140.5 1.9 copy-start.14
  170.8 1.0 copy-start.10
  175.4 1.0 copy-start.7
  175.4 1.2 copy-start.9
  176.1 9.9 %copy-start.12 = (f32[9,32,32]{2,1,0:T(8,128)S(1)}, f32[9,32,32]{2,1,0:T(8,128)}, u32[]{:S(2)}) copy-start(f32[9,32,32]{2,1,0:T(8,128)} %param.31) | copy-start | bytes 110596
  177.4 5.4 %collective-permute-start = (f32[32,1,128]{2,0,1:T(8,128)S(1)}, f32[32,1,128]{2,0,1:T(8,128)S(1)}, u32[]{:S(2)}, u32[]{:S(2)}) collective-permute-start(f32[32,1,128]{2,0,1:T(8,128)S(1)} %get-tuple-element.23), channel_id=1, source_target_pairs={{0,1},{1,2},{2,3},{3,4},{4,5},{5,6},{6,7},{7,8},{8,9},{9,10},{10,1... | collective-permute-start | bytes 49160 | tf_op jit(solution)/shard_map/ppermute | solution.py:20
  180.6 5.1 %collective-permute-start.1 = (f32[32,1,128]{2,0,1:T(8,128)S(1)}, f32[32,1,128]{2,0,1:T(8,128)S(1)}, u32[]{:S(2)}, u32[]{:S(2)}) collective-permute-start(f32[32,1,128]{2,0,1:T(8,128)S(1)} %get-tuple-element.24), channel_id=1, source_target_pairs={{1,0},{2,1},{3,2},{4,3},{5,4},{6,5},{7,6},{8,7},{9,8},{10,9},{11,1... | collective-permute-start | bytes 49160 | tf_op jit(solution)/shard_map/ppermute | solution.py:23
  188.6 2.5 %copy-start.8 = (f32[32,32,128]{2,1,0:T(8,128)S(1)}, f32[32,32,128]{2,1,0:T(8,128)}, u32[]{:S(2)}) copy-start(f32[32,32,128]{2,1,0:T(8,128)} %param.18) | copy-start | bytes 1572868
  190.4 3.7 %copy-start.1 = (bf16[128,2048]{1,0:T(8,128)(2,1)S(1)}, bf16[128,2048]{1,0:T(8,128)(2,1)}, u32[]{:S(2)}) copy-start(bf16[128,2048]{1,0:T(8,128)(2,1)} %param.22) | copy-start | bytes 1572868
Sparse Core Ops, SparseCore 0:
  11.5 98.4 all-gather.4
  112.1 51.4 all-gather.6
